TPU v7x, 512 devices: a whole 4x8x8 slice. The times are simulated.
512 devices in a mesh: region: 8 (over z), sub: 64 (over y, x, core).
Axes of the slice: x: 4, y: 8, z: 8, core: 2. Of those that a mesh axis runs over, the one named last changes fastest.
Arguments:
- right_side: bfloat16 [8, 64, 1024, 256], P('region', 'sub'), may hold values from -6 to 6
- local_inverse: bfloat16 [8, 64, 1024, 1024], P('region', 'sub')
- coupling: bfloat16 [8, 64, 4, 256, 256], P('region', 'sub'), may hold values from -0.75 to 0.75
- margin_blocks: int32 [4, 8, 64, 2], P(None, 'region', 'sub'), may hold values from 0 to 7, as said below
- partner: int32 [4, 512], replicated, may hold values from 0 to 511, as said below
- restriction: bfloat16 [8, 64, 64, 1024], P('region', 'sub'), may hold values from -0.375 to 0.375
- coarse_rows: bfloat16 [8, 4096, 4096], P('region', 'sub')
Outputs:
- solution: bfloat16 [8, 64, 1024, 256], P('region', 'sub')
Inputs may be any that keep to these rules, and one draw needn't show every extreme that they name: `margin_blocks`: for each colour, subdomain and k, a block number below 8; the 2 numbers of one colour and subdomain are distinct. For each colour a perfect matching of all subdomains: the partner of a subdomain's partner is the subdomain itself, and no subdomain is its own partner.
All inputs are finite; a program needn't handle non-finite values.
Results may differ from a plain program's by a relative error of at most 0.0052.
Values may be sent and summed in bfloat16 or wider, within the bound.
No kernel may reach another device: no remote copies, remote signals or barrier semaphores. Data moves between devices by JAX's collectives and lax.ppermute only.
A program may use at most 64 MiB of HBM per device.

v0:
```python
import jax
import jax.numpy as jnp
from jax import lax
from jax.sharding import PartitionSpec as P

BLK = 128
OVL_BLK = 2
COLORS = 4


def rows_of(matrix, picked):
    return jnp.concatenate(
        [lax.dynamic_slice_in_dim(matrix, picked[k] * BLK, BLK, axis=0) for k in range(OVL_BLK)],
        axis=0,
    )


def exchange(sent_rows, mates, all_peers):
    span_rows, columns = sent_rows.shape
    pieces = sent_rows.reshape(all_peers, span_rows * columns // all_peers)
    relayed = lax.all_to_all(pieces, ("region", "sub"), 0, 0, tiled=True)
    relayed = jnp.take(relayed, mates, axis=0)
    returned = lax.all_to_all(relayed, ("region", "sub"), 0, 0, tiled=True)
    return returned.reshape(span_rows, columns)


def shards(right_side, local_inverse, coupling, margin_blocks, partner, restriction, coarse_rows):
    inverse = local_inverse[0, 0]
    tile_set = coupling[0, 0]
    own_blocks = margin_blocks[:, 0, 0, :]
    columns = right_side.shape[-1]
    sub_peers = lax.axis_size("sub")
    all_peers = sub_peers * lax.axis_size("region")
    residual = right_side[0, 0].astype(jnp.float32)
    accumulated = None
    sent_rows = rows_of(right_side[0, 0], own_blocks[0])
    for colour in range(COLORS):
        picked = own_blocks[colour]
        received = exchange(sent_rows, partner[colour], all_peers)
        coupled = jnp.dot(tile_set[colour], received, preferred_element_type=jnp.float32)
        widened = residual
        for k in range(OVL_BLK):
            start = picked[k] * BLK
            block = lax.dynamic_slice_in_dim(widened, start, BLK, axis=0)
            widened = lax.dynamic_update_slice_in_dim(
                widened, block + coupled[k * BLK:(k + 1) * BLK], start, axis=0
            )
        shaped = widened.astype(jnp.bfloat16)
        if colour + 1 < COLORS:
            upcoming = own_blocks[colour + 1]
            ahead = jnp.dot(rows_of(inverse, upcoming), shaped, preferred_element_type=jnp.float32)
            sent_rows = (rows_of(widened, upcoming) - 0.25 * ahead).astype(jnp.bfloat16)
        correction = jnp.dot(inverse, shaped, preferred_element_type=jnp.float32)
        accumulated = correction if accumulated is None else accumulated + correction
        residual = widened - 0.25 * correction
    settled = residual.astype(jnp.bfloat16)
    own_restriction = restriction[0, 0]
    projected = jnp.dot(own_restriction, settled, preferred_element_type=jnp.float32).astype(
        jnp.bfloat16
    )
    copies = jnp.broadcast_to(projected[None], (sub_peers,) + projected.shape)
    gathered = lax.all_to_all(copies, "sub", 0, 0, tiled=True).reshape(-1, columns)
    coarse = jnp.dot(coarse_rows[0], gathered, preferred_element_type=jnp.float32).astype(
        jnp.bfloat16
    )
    lifted = lax.dot_general(
        own_restriction, coarse, (((0,), (0,)), ((), ())), preferred_element_type=jnp.float32
    )
    return (accumulated + lifted).astype(jnp.bfloat16)[None, None]


def solution(mesh):
    placed = (
        P("region", "sub", None, None),
        P("region", "sub", None, None),
        P("region", "sub", None, None, None),
        P(None, "region", "sub", None),
        P(),
        P("region", "sub", None, None),
        P("region", "sub", None),
    )
    return jax.shard_map(
        shards,
        mesh=mesh,
        in_specs=placed,
        out_specs=P("region", "sub", None, None),
        check_vma=False,
    )
```

profile of v0, /device:TPU:1, one launch (start us, length us, event | category | flops | bytes accessed | tf_op | source)
XLA Modules:
  0.0 337.5 jit_solution(4789033435722386834)
XLA Ops:
  0.0 1.7 fusion.62
  4.6 22.1 %all-to-all-start = ((bf16[512,1,128]{2,1,0:T(2,128)(2,1)}), bf16[512,1,128]{2,1,0:T(2,128)(2,1)S(1)}, u32[]{:S(2)}, u32[]{:S(2)}) async-start(bf16[512,1,128]{2,1,0:T(2,128)(2,1)} %all_to_all.80), calls=%async_computation | async-start | bytes 524288 | tf_op jit(solution)/shard_map/all_to_all | solution.py:21
  32.0 2.3 dynamic-slice_bitcast_fusion.1
  34.8 9.3 %all-to-all-done = bf16[512,1,128]{2,1,0:T(2,128)(2,1)S(1)} async-done(((bf16[512,1,128]{2,1,0:T(2,128)(2,1)}), bf16[512,1,128]{2,1,0:T(2,128)(2,1)S(1)}, u32[]{:S(2)}, u32[]{:S(2)}) %all-to-all-start) | async-done | bytes 131104 | tf_op jit(solution)/shard_map/all_to_all | solution.py:21
  44.1 1.3 gather_fusion
  46.5 10.0 %all-to-all-start.1 = ((bf16[512,1,128]{2,1,0:T(2,128)(2,1)}), bf16[512,1,128]{2,1,0:T(2,128)(2,1)S(1)}, u32[]{:S(2)}, u32[]{:S(2)}) async-start(bf16[512,1,128]{2,1,0:T(2,128)(2,1)} %copy.28), calls=%async_computation.1 | async-start | bytes 524288 | tf_op jit(solution)/shard_map/all_to_all | solution.py:23
  56.6 1.5 fusion.60
  58.1 15.9 %all-to-all-done.1 = bf16[512,1,128]{2,1,0:T(2,128)(2,1)S(1)} async-done(((bf16[512,1,128]{2,1,0:T(2,128)(2,1)}), bf16[512,1,128]{2,1,0:T(2,128)(2,1)S(1)}, u32[]{:S(2)}, u32[]{:S(2)}) %all-to-all-start.1) | async-done | bytes 131104 | tf_op jit(solution)/shard_map/all_to_all | solution.py:23
  75.9 1.7 fusion.45
  77.6 1.6 fusion.44
  80.2 1.7 fusion.15
  82.6 11.0 %all-to-all-start.2 = ((bf16[512,1,128]{2,1,0:T(2,128)(2,1)}), bf16[512,1,128]{2,1,0:T(2,128)(2,1)}, u32[]{:S(2)}, u32[]{:S(2)}) async-start(bf16[512,1,128]{2,1,0:T(2,128)(2,1)} %all_to_all.81), calls=%async_computation.2 | async-start | bytes 524288 | tf_op jit(solution)/shard_map/all_to_all | solution.py:21
  93.7 3.0 fusion.6
  96.7 2.6 copy.29
  99.2 10.3 %all-to-all-done.2 = bf16[512,1,128]{2,1,0:T(2,128)(2,1)} async-done(((bf16[512,1,128]{2,1,0:T(2,128)(2,1)}), bf16[512,1,128]{2,1,0:T(2,128)(2,1)}, u32[]{:S(2)}, u32[]{:S(2)}) %all-to-all-start.2) | async-done | bytes 131104 | tf_op jit(solution)/shard_map/all_to_all | solution.py:21
  110.5 1.9 gather_fusion.1
  114.4 11.2 %all-to-all-start.3 = ((bf16[512,1,128]{2,1,0:T(2,128)(2,1)}), bf16[512,1,128]{2,1,0:T(2,128)(2,1)}, u32[]{:S(2)}, u32[]{:S(2)}) async-start(bf16[512,1,128]{2,1,0:T(2,128)(2,1)} %copy.31), calls=%async_computation.3 | async-start | bytes 524288 | tf_op jit(solution)/shard_map/all_to_all | solution.py:23
  125.6 2.7 bitcast_subtract_fusion.3
  128.3 13.3 %all-to-all-done.3 = bf16[512,1,128]{2,1,0:T(2,128)(2,1)} async-done(((bf16[512,1,128]{2,1,0:T(2,128)(2,1)}), bf16[512,1,128]{2,1,0:T(2,128)(2,1)}, u32[]{:S(2)}, u32[]{:S(2)}) %all-to-all-start.3) | async-done | bytes 131104 | tf_op jit(solution)/shard_map/all_to_all | solution.py:23
  141.6 1.7 reduce.1
  145.1 1.6 fusion.43
  146.7 1.6 fusion.42
  149.2 1.6 fusion.14
  151.6 8.6 %all-to-all-start.4 = ((bf16[512,1,128]{2,1,0:T(2,128)(2,1)}), bf16[512,1,128]{2,1,0:T(2,128)(2,1)S(1)}, u32[]{:S(2)}, u32[]{:S(2)}) async-start(bf16[512,1,128]{2,1,0:T(2,128)(2,1)} %all_to_all.82), calls=%async_computation.4 | async-start | bytes 524288 | tf_op jit(solution)/shard_map/all_to_all | solution.py:21
  160.2 3.0 fusion.4
  163.2 2.6 copy.32
  165.8 12.0 %all-to-all-done.4 = bf16[512,1,128]{2,1,0:T(2,128)(2,1)S(1)} async-done(((bf16[512,1,128]{2,1,0:T(2,128)(2,1)}), bf16[512,1,128]{2,1,0:T(2,128)(2,1)S(1)}, u32[]{:S(2)}, u32[]{:S(2)}) %all-to-all-start.4) | async-done | bytes 131104 | tf_op jit(solution)/shard_map/all_to_all | solution.py:21
  177.7 1.3 gather_fusion.2
  180.2 8.4 %all-to-all-start.5 = ((bf16[512,1,128]{2,1,0:T(2,128)(2,1)}), bf16[512,1,128]{2,1,0:T(2,128)(2,1)S(1)}, u32[]{:S(2)}, u32[]{:S(2)}) async-start(bf16[512,1,128]{2,1,0:T(2,128)(2,1)} %copy.34), calls=%async_computation.5 | async-start | bytes 524288 | tf_op jit(solution)/shard_map/all_to_all | solution.py:23
  188.5 2.7 bitcast_subtract_fusion.2
  191.2 14.8 %all-to-all-done.5 = bf16[512,1,128]{2,1,0:T(2,128)(2,1)S(1)} async-done(((bf16[512,1,128]{2,1,0:T(2,128)(2,1)}), bf16[512,1,128]{2,1,0:T(2,128)(2,1)S(1)}, u32[]{:S(2)}, u32[]{:S(2)}) %all-to-all-start.5) | async-done | bytes 131104 | tf_op jit(solution)/shard_map/all_to_all | solution.py:23
  207.9 1.6 fusion.41
  209.5 1.6 fusion.40
  212.1 1.5 fusion.13
  214.4 8.6 %all-to-all-start.6 = ((bf16[512,1,128]{2,1,0:T(2,128)(2,1)}), bf16[512,1,128]{2,1,0:T(2,128)(2,1)S(1)}, u32[]{:S(2)}, u32[]{:S(2)}) async-start(bf16[512,1,128]{2,1,0:T(2,128)(2,1)} %all_to_all.83), calls=%async_computation.6 | async-start | bytes 524288 | tf_op jit(solution)/shard_map/all_to_all | solution.py:21
  223.0 3.0 fusion.2
  226.0 2.5 copy.35
  228.5 12.0 %all-to-all-done.6 = bf16[512,1,128]{2,1,0:T(2,128)(2,1)S(1)} async-done(((bf16[512,1,128]{2,1,0:T(2,128)(2,1)}), bf16[512,1,128]{2,1,0:T(2,128)(2,1)S(1)}, u32[]{:S(2)}, u32[]{:S(2)}) %all-to-all-start.6) | async-done | bytes 131104 | tf_op jit(solution)/shard_map/all_to_all | solution.py:21
  240.5 1.3 gather_fusion.3
  242.9 8.4 %all-to-all-start.7 = ((bf16[512,1,128]{2,1,0:T(2,128)(2,1)}), bf16[512,1,128]{2,1,0:T(2,128)(2,1)S(1)}, u32[]{:S(2)}, u32[]{:S(2)}) async-start(bf16[512,1,128]{2,1,0:T(2,128)(2,1)} %copy.37), calls=%async_computation.7 | async-start | bytes 524288 | tf_op jit(solution)/shard_map/all_to_all | solution.py:23
  251.3 2.7 bitcast_subtract_fusion.1
  254.0 14.8 %all-to-all-done.7 = bf16[512,1,128]{2,1,0:T(2,128)(2,1)S(1)} async-done(((bf16[512,1,128]{2,1,0:T(2,128)(2,1)}), bf16[512,1,128]{2,1,0:T(2,128)(2,1)S(1)}, u32[]{:S(2)}, u32[]{:S(2)}) %all-to-all-start.7) | async-done | bytes 131104 | tf_op jit(solution)/shard_map/all_to_all | solution.py:23
  270.7 1.6 fusion.39
  272.3 1.6 fusion.38
  273.9 3.0 fusion
  276.9 1.6 copy.39
  279.1 54.2 %all_to_all.93 = bf16[64,64,256]{2,1,0:T(8,128)(2,1)} all-to-all(bf16[64,64,256]{2,1,0:T(8,128)(2,1)S(1)} %broadcast_in_dim.18), channel_id=1, replica_groups=mesh['region'=8,'sub'=64] {'sub'}, dimensions={0} | all-to-all | bytes 4194304 | tf_op jit(solution)/shard_map/all_to_all | solution.py:62
  333.3 3.2 fusion.9
  (64 shorter events, 24.0 us)
Async XLA Ops:
  0.0 333.3 %copy-start = (bf16[1,64,4096]{2,1,0:T(8,128)(2,1)S(1)}, bf16[1,64,4096]{2,1,0:T(8,128)(2,1)}, u32[]{:S(2)}) copy-start(bf16[1,64,4096]{2,1,0:T(8,128)(2,1)} %param.15) | copy-start | bytes 1572868
  4.6 39.5 %all-to-all-start = ((bf16[512,1,128]{2,1,0:T(2,128)(2,1)}), bf16[512,1,128]{2,1,0:T(2,128)(2,1)S(1)}, u32[]{:S(2)}, u32[]{:S(2)}) async-start(bf16[512,1,128]{2,1,0:T(2,128)(2,1)} %all_to_all.80), calls=%async_computation | async-start | bytes 524288 | tf_op jit(solution)/shard_map/all_to_all | solution.py:21
  34.3 22.3 %copy-start.5 = (bf16[1,1,1024,256]{3,2,1,0:T(8,128)(2,1)S(1)}, bf16[1,1,1024,256]{3,2,1,0:T(8,128)(2,1)}, u32[]{:S(2)}) copy-start(bf16[1,1,1024,256]{3,2,1,0:T(8,128)(2,1)} %param.9) | copy-start | bytes 1572868
  46.5 27.4 %all-to-all-start.1 = ((bf16[512,1,128]{2,1,0:T(2,128)(2,1)}), bf16[512,1,128]{2,1,0:T(2,128)(2,1)S(1)}, u32[]{:S(2)}, u32[]{:S(2)}) async-start(bf16[512,1,128]{2,1,0:T(2,128)(2,1)} %copy.28), calls=%async_computation.1 | async-start | bytes 524288 | tf_op jit(solution)/shard_map/all_to_all | solution.py:23
  75.9 17.8 %copy-start.1 = (bf16[1,1,1024,1024]{3,2,1,0:T(8,128)(2,1)S(1)}, bf16[1,1,1024,1024]{3,2,1,0:T(8,128)(2,1)}, u32[]{:S(2)}) copy-start(bf16[1,1,1024,1024]{3,2,1,0:T(8,128)(2,1)} %param.10) | copy-start | bytes 6291460
  82.6 26.9 %all-to-all-start.2 = ((bf16[512,1,128]{2,1,0:T(2,128)(2,1)}), bf16[512,1,128]{2,1,0:T(2,128)(2,1)}, u32[]{:S(2)}, u32[]{:S(2)}) async-start(bf16[512,1,128]{2,1,0:T(2,128)(2,1)} %all_to_all.81), calls=%async_computation.2 | async-start | bytes 524288 | tf_op jit(solution)/shard_map/all_to_all | solution.py:21
  114.4 27.2 %all-to-all-start.3 = ((bf16[512,1,128]{2,1,0:T(2,128)(2,1)}), bf16[512,1,128]{2,1,0:T(2,128)(2,1)}, u32[]{:S(2)}, u32[]{:S(2)}) async-start(bf16[512,1,128]{2,1,0:T(2,128)(2,1)} %copy.31), calls=%async_computation.3 | async-start | bytes 524288 | tf_op jit(solution)/shard_map/all_to_all | solution.py:23
  151.6 26.1 %all-to-all-start.4 = ((bf16[512,1,128]{2,1,0:T(2,128)(2,1)}), bf16[512,1,128]{2,1,0:T(2,128)(2,1)S(1)}, u32[]{:S(2)}, u32[]{:S(2)}) async-start(bf16[512,1,128]{2,1,0:T(2,128)(2,1)} %all_to_all.82), calls=%async_computation.4 | async-start | bytes 524288 | tf_op jit(solution)/shard_map/all_to_all | solution.py:21
  163.2 15.9 %copy-start.7 = (pred[512]{0:T(512)(128)(4,1)S(1)}, pred[512]{0:T(512)(128)(4,1)}, u32[]{:S(2)}) copy-start(pred[512]{0:T(512)(128)(4,1)} %compare_and_fusion.1) | copy-start | bytes 1540
  180.2 25.9 %all-to-all-start.5 = ((bf16[512,1,128]{2,1,0:T(2,128)(2,1)}), bf16[512,1,128]{2,1,0:T(2,128)(2,1)S(1)}, u32[]{:S(2)}, u32[]{:S(2)}) async-start(bf16[512,1,128]{2,1,0:T(2,128)(2,1)} %copy.34), calls=%async_computation.5 | async-start | bytes 524288 | tf_op jit(solution)/shard_map/all_to_all | solution.py:23
  214.4 26.1 %all-to-all-start.6 = ((bf16[512,1,128]{2,1,0:T(2,128)(2,1)}), bf16[512,1,128]{2,1,0:T(2,128)(2,1)S(1)}, u32[]{:S(2)}, u32[]{:S(2)}) async-start(bf16[512,1,128]{2,1,0:T(2,128)(2,1)} %all_to_all.83), calls=%async_computation.6 | async-start | bytes 524288 | tf_op jit(solution)/shard_map/all_to_all | solution.py:21
  242.9 25.9 %all-to-all-start.7 = ((bf16[512,1,128]{2,1,0:T(2,128)(2,1)}), bf16[512,1,128]{2,1,0:T(2,128)(2,1)S(1)}, u32[]{:S(2)}, u32[]{:S(2)}) async-start(bf16[512,1,128]{2,1,0:T(2,128)(2,1)} %copy.37), calls=%async_computation.7 | async-start | bytes 524288 | tf_op jit(solution)/shard_map/all_to_all | solution.py:23
  276.9 1.7 copy-start.2
  276.9 1.7 copy-start.6
  279.0 54.3 %copy-start.3 = (f32[256,1024]{1,0:T(8,128)S(1)}, f32[256,1024]{1,0:T(8,128)}, u32[]{:S(2)}) copy-start(f32[256,1024]{1,0:T(8,128)} %fusion.6) | copy-start | bytes 3145732
  279.1 54.3 %copy-start.4 = (f32[256,1024]{1,0:T(8,128)S(1)}, f32[256,1024]{1,0:T(8,128)}, u32[]{:S(2)}) copy-start(f32[256,1024]{1,0:T(8,128)} %fusion.4) | copy-start | bytes 3145732
where the time goes:
time: 339 us; the launch traced here: 338 us
  waiting for transfers between devices  102 us (30%)
  starting transfers between devices  88.4 us (26%)
  blocking collectives  54.2 us (16%)
  local copies, waits for them, and re-layouts  33.7 us (10%)
  other arithmetic  28.7 us (8%)
  matrix products  24.6 us (7%)
  between operations  5.45 us (2%)
    all_to_all x4, waiting for transfers between devices, exchange(): returned = lax.all_to_all(relayed, ('region', 'sub'), 0, 0, tiled=True)  58.8 us
    all_to_all x1, blocking collectives, shards(): lax.all_to_all(copies, 'sub', 0, 0, tiled=True).reshape(-1, columns)  54.2 us
    all_to_all x4, starting transfers between devices, exchange(): relayed = lax.all_to_all(pieces, ('region', 'sub'), 0, 0, tiled=True)  50.4 us
    all_to_all x4, waiting for transfers between devices, exchange(): relayed = lax.all_to_all(pieces, ('region', 'sub'), 0, 0, tiled=True)  43.6 us
    all_to_all x4, starting transfers between devices, exchange(): returned = lax.all_to_all(relayed, ('region', 'sub'), 0, 0, tiled=True)  38 us
    dynamic_update_slice x8, other arithmetic, shards(): lax.dynamic_update_slice_in_dim(widened, block + coupled[k * BLK:(k + 1)...  12.8 us
    dot_general x4, matrix products, shards(): correction = jnp.dot(inverse, shaped, preferred_element_type=jnp.float32)  11.9 us
    dot_general x4, local copies, waits for them, and re-layouts, shards(): correction = jnp.dot(inverse, shaped, preferred_element_type=jnp.float32)  9.3 us
  transfers between devices with their start and end apart: 8, of which 8 were waited for; matrix products, arithmetic and copies ran while one was open for 9% of the time, Pallas kernels for 0%

commit v1 on v0

--- a/solution.py
+++ b/solution.py
@@ -37,19 +37,29 @@
     for colour in range(COLORS):
         picked = own_blocks[colour]
         received = exchange(sent_rows, partner[colour], all_peers)
+        base = residual.astype(jnp.bfloat16)
+        if colour + 1 < COLORS:
+            next_inverse_rows = rows_of(inverse, own_blocks[colour + 1])
+            next_residual_rows = rows_of(residual, own_blocks[colour + 1])
         coupled = jnp.dot(tile_set[colour], received, preferred_element_type=jnp.float32)
+        parts = [coupled[k * BLK:(k + 1) * BLK] for k in range(OVL_BLK)]
         widened = residual
+        shaped = base
         for k in range(OVL_BLK):
             start = picked[k] * BLK
-            block = lax.dynamic_slice_in_dim(widened, start, BLK, axis=0)
-            widened = lax.dynamic_update_slice_in_dim(
-                widened, block + coupled[k * BLK:(k + 1) * BLK], start, axis=0
-            )
-        shaped = widened.astype(jnp.bfloat16)
+            block = lax.dynamic_slice_in_dim(residual, start, BLK, axis=0) + parts[k]
+            widened = lax.dynamic_update_slice_in_dim(widened, block, start, axis=0)
+            shaped = lax.dynamic_update_slice_in_dim(shaped, block.astype(jnp.bfloat16), start, axis=0)
         if colour + 1 < COLORS:
             upcoming = own_blocks[colour + 1]
-            ahead = jnp.dot(rows_of(inverse, upcoming), shaped, preferred_element_type=jnp.float32)
-            sent_rows = (rows_of(widened, upcoming) - 0.25 * ahead).astype(jnp.bfloat16)
+            ahead = jnp.dot(next_inverse_rows, shaped, preferred_element_type=jnp.float32)
+            near = []
+            for j in range(OVL_BLK):
+                row = next_residual_rows[j * BLK:(j + 1) * BLK]
+                for k in range(OVL_BLK):
+                    row = jnp.where(upcoming[j] == picked[k], row + parts[k], row)
+                near.append(row)
+            sent_rows = (jnp.concatenate(near, axis=0) - 0.25 * ahead).astype(jnp.bfloat16)
         correction = jnp.dot(inverse, shaped, preferred_element_type=jnp.float32)
         accumulated = correction if accumulated is None else accumulated + correction
         residual = widened - 0.25 * correction

time: 339 us -> 349 us (1.029)
  waiting for transfers between devices: 102 us -> 83.3 us
  between operations: 5.45 us -> 20.3 us
  starting transfers between devices: 88.4 us -> 101 us
  matrix products: 24.6 us -> 16 us
  local copies, waits for them, and re-layouts: 33.7 us -> 38.9 us
  other arithmetic: 28.7 us -> 33.1 us
    all_to_all x4, waiting for transfers between devices: 58.8 us -> 41.2 us  [exchange(): returned = lax.all_to_all(relayed, ('region', 'sub'), 0, 0, tiled=True)]
    all_to_all x4, starting transfers between devices: 50.4 us -> 63.6 us  [exchange(): relayed = lax.all_to_all(pieces, ('region', 'sub'), 0, 0, tiled=True)]
    unnamed x20 -> x47, local copies, waits for them, and re-layouts: 1.06 us -> 11.3 us
    sub x3 -> x0, other arithmetic: 8.01 us -> none  [shards(): residual = widened - 0.25 * correction]
    select_n x0 -> x3, other arithmetic: none -> 5.22 us  [shards(): row = jnp.where(upcoming[j] == picked[k], row + parts[k], row)]
    convert_element_type x0 -> x3, other arithmetic: none -> 5.19 us  [shards(): base = residual.astype(jnp.bfloat16)]
    dynamic_slice x5 -> x2, local copies, waits for them, and re-layouts: 6.16 us -> 1.19 us  [rows_of(): lax.dynamic_slice_in_dim(matrix, picked[k] * BLK, BLK, axis=0)]
    dot_general x4, matrix products: 11.9 us -> 7.06 us  [shards(): correction = jnp.dot(inverse, shaped, preferred_element_type=jnp.float32)]
  transfers between devices with their start and end apart: 8 -> 8, of which waited for: 8 -> 7; matrix products, arithmetic and copies ran while one was open for 9% -> 9% of each run, Pallas kernels for 0% -> 0%
where the time goes in v1:
time: 349 us; the launch traced here: 347 us
  starting transfers between devices  101 us (29%)
  waiting for transfers between devices  83.3 us (24%)
  blocking collectives  54.2 us (16%)
  local copies, waits for them, and re-layouts  38.9 us (11%)
  other arithmetic  33.1 us (9%)
  between operations  20.3 us (6%)
  matrix products  16 us (5%)
    all_to_all x4, starting transfers between devices, exchange(): relayed = lax.all_to_all(pieces, ('region', 'sub'), 0, 0, tiled=True)  63.6 us
    all_to_all x1, blocking collectives, shards(): lax.all_to_all(copies, 'sub', 0, 0, tiled=True).reshape(-1, columns)  54.2 us
    all_to_all x4, waiting for transfers between devices, exchange(): relayed = lax.all_to_all(pieces, ('region', 'sub'), 0, 0, tiled=True)  42.1 us
    all_to_all x4, waiting for transfers between devices, exchange(): returned = lax.all_to_all(relayed, ('region', 'sub'), 0, 0, tiled=True)  41.2 us
    all_to_all x4, starting transfers between devices, exchange(): returned = lax.all_to_all(relayed, ('region', 'sub'), 0, 0, tiled=True)  37.5 us
    unnamed x47, local copies, waits for them, and re-layouts  11.3 us
    dot_general x4, local copies, waits for them, and re-layouts, shards(): correction = jnp.dot(inverse, shaped, preferred_element_type=jnp.float32)  9.35 us
    dynamic_update_slice x8, other arithmetic, shards(): lax.dynamic_update_slice_in_dim(shaped, block.astype(jnp.bfloat16), start...  7.44 us
  transfers between devices with their start and end apart: 8, of which 7 were waited for; matrix products, arithmetic and copies ran while one was open for 9% of the time, Pallas kernels for 0%

profile of v1, /device:TPU:1, one launch (start us, length us, event | category | flops | bytes accessed | tf_op | source)
XLA Modules:
  0.0 346.9 jit_solution(547372274043590551)
XLA Ops:
  0.0 1.2 copy.71
  1.2 1.6 fusion.56
  4.9 22.1 %all-to-all-start = ((bf16[512,1,128]{2,1,0:T(2,128)(2,1)}), bf16[512,1,128]{2,1,0:T(2,128)(2,1)S(1)}, u32[]{:S(2)}, u32[]{:S(2)}) async-start(bf16[512,1,128]{2,1,0:T(2,128)(2,1)} %all_to_all.80), calls=%async_computation | async-start | bytes 524288 | tf_op jit(solution)/shard_map/all_to_all | solution.py:21
  33.1 1.2 dynamic-slice_bitcast_fusion.1
  34.3 1.1 bitcast_convert_fusion
  35.4 9.1 %all-to-all-done = bf16[512,1,128]{2,1,0:T(2,128)(2,1)S(1)} async-done(((bf16[512,1,128]{2,1,0:T(2,128)(2,1)}), bf16[512,1,128]{2,1,0:T(2,128)(2,1)S(1)}, u32[]{:S(2)}, u32[]{:S(2)}) %all-to-all-start) | async-done | bytes 131104 | tf_op jit(solution)/shard_map/all_to_all | solution.py:21
  44.5 1.3 gather_fusion
  47.5 10.3 %all-to-all-start.1 = ((bf16[512,1,128]{2,1,0:T(2,128)(2,1)}), bf16[512,1,128]{2,1,0:T(2,128)(2,1)S(1)}, u32[]{:S(2)}, u32[]{:S(2)}) async-start(bf16[512,1,128]{2,1,0:T(2,128)(2,1)} %copy.28), calls=%async_computation.1 | async-start | bytes 524288 | tf_op jit(solution)/shard_map/all_to_all | solution.py:23
  73.3 2.3 copy.54
  77.0 1.1 convolution_bitcast_fusion.3
  80.1 1.6 fusion.41
  81.7 1.7 add_select_fusion.10
  84.5 19.4 %all-to-all-start.2 = ((bf16[512,1,128]{2,1,0:T(2,128)(2,1)}), bf16[512,1,128]{2,1,0:T(2,128)(2,1)S(1)}, u32[]{:S(2)}, u32[]{:S(2)}) async-start(bf16[512,1,128]{2,1,0:T(2,128)(2,1)} %all_to_all.81), calls=%async_computation.2 | async-start | bytes 524288 | tf_op jit(solution)/shard_map/all_to_all | solution.py:21
  103.8 1.8 fusion.6
  105.6 2.5 copy.29
  108.1 13.1 %all-to-all-done.2 = bf16[512,1,128]{2,1,0:T(2,128)(2,1)S(1)} async-done(((bf16[512,1,128]{2,1,0:T(2,128)(2,1)}), bf16[512,1,128]{2,1,0:T(2,128)(2,1)S(1)}, u32[]{:S(2)}, u32[]{:S(2)}) %all-to-all-start.2) | async-done | bytes 131104 | tf_op jit(solution)/shard_map/all_to_all | solution.py:21
  121.2 1.3 gather_fusion.1
  123.6 8.4 %all-to-all-start.3 = ((bf16[512,1,128]{2,1,0:T(2,128)(2,1)}), bf16[512,1,128]{2,1,0:T(2,128)(2,1)S(1)}, u32[]{:S(2)}, u32[]{:S(2)}) async-start(bf16[512,1,128]{2,1,0:T(2,128)(2,1)} %copy.31), calls=%async_computation.3 | async-start | bytes 524288 | tf_op jit(solution)/shard_map/all_to_all | solution.py:23
  132.0 1.7 fusion.54
  135.7 13.8 %all-to-all-done.3 = bf16[512,1,128]{2,1,0:T(2,128)(2,1)S(1)} async-done(((bf16[512,1,128]{2,1,0:T(2,128)(2,1)}), bf16[512,1,128]{2,1,0:T(2,128)(2,1)S(1)}, u32[]{:S(2)}, u32[]{:S(2)}) %all-to-all-start.3) | async-done | bytes 131104 | tf_op jit(solution)/shard_map/all_to_all | solution.py:23
  151.0 1.2 convolution_bitcast_fusion.2
  154.0 1.7 add_select_fusion.6
  156.9 11.1 %all-to-all-start.4 = ((bf16[512,1,128]{2,1,0:T(2,128)(2,1)}), bf16[512,1,128]{2,1,0:T(2,128)(2,1)}, u32[]{:S(2)}, u32[]{:S(2)}) async-start(bf16[512,1,128]{2,1,0:T(2,128)(2,1)} %all_to_all.82), calls=%async_computation.4 | async-start | bytes 524288 | tf_op jit(solution)/shard_map/all_to_all | solution.py:21
  167.9 1.7 fusion.4
  169.7 2.6 copy.32
  172.3 1.6 fusion.44
  173.8 10.0 %all-to-all-done.4 = bf16[512,1,128]{2,1,0:T(2,128)(2,1)} async-done(((bf16[512,1,128]{2,1,0:T(2,128)(2,1)}), bf16[512,1,128]{2,1,0:T(2,128)(2,1)}, u32[]{:S(2)}, u32[]{:S(2)}) %all-to-all-start.4) | async-done | bytes 131104 | tf_op jit(solution)/shard_map/all_to_all | solution.py:21
  184.8 1.3 gather_fusion.2
  187.2 9.4 %all-to-all-start.5 = ((bf16[512,1,128]{2,1,0:T(2,128)(2,1)}), bf16[512,1,128]{2,1,0:T(2,128)(2,1)S(1)}, u32[]{:S(2)}, u32[]{:S(2)}) async-start(bf16[512,1,128]{2,1,0:T(2,128)(2,1)} %copy.34), calls=%async_computation.5 | async-start | bytes 524288 | tf_op jit(solution)/shard_map/all_to_all | solution.py:23
  196.6 1.7 fusion.53
  200.3 13.7 %all-to-all-done.5 = bf16[512,1,128]{2,1,0:T(2,128)(2,1)S(1)} async-done(((bf16[512,1,128]{2,1,0:T(2,128)(2,1)}), bf16[512,1,128]{2,1,0:T(2,128)(2,1)S(1)}, u32[]{:S(2)}, u32[]{:S(2)}) %all-to-all-start.5) | async-done | bytes 131104 | tf_op jit(solution)/shard_map/all_to_all | solution.py:23
  215.5 1.2 convolution_bitcast_fusion.1
  218.5 1.8 add_select_fusion.2
  221.4 11.1 %all-to-all-start.6 = ((bf16[512,1,128]{2,1,0:T(2,128)(2,1)}), bf16[512,1,128]{2,1,0:T(2,128)(2,1)}, u32[]{:S(2)}, u32[]{:S(2)}) async-start(bf16[512,1,128]{2,1,0:T(2,128)(2,1)} %all_to_all.83), calls=%async_computation.6 | async-start | bytes 524288 | tf_op jit(solution)/shard_map/all_to_all | solution.py:21
  232.4 1.8 fusion.2
  234.2 2.6 copy.35
  236.8 1.6 fusion.46
  238.4 10.0 %all-to-all-done.6 = bf16[512,1,128]{2,1,0:T(2,128)(2,1)} async-done(((bf16[512,1,128]{2,1,0:T(2,128)(2,1)}), bf16[512,1,128]{2,1,0:T(2,128)(2,1)}, u32[]{:S(2)}, u32[]{:S(2)}) %all-to-all-start.6) | async-done | bytes 131104 | tf_op jit(solution)/shard_map/all_to_all | solution.py:21
  249.3 1.3 gather_fusion.3
  251.7 9.4 %all-to-all-start.7 = ((bf16[512,1,128]{2,1,0:T(2,128)(2,1)}), bf16[512,1,128]{2,1,0:T(2,128)(2,1)S(1)}, u32[]{:S(2)}, u32[]{:S(2)}) async-start(bf16[512,1,128]{2,1,0:T(2,128)(2,1)} %copy.37), calls=%async_computation.7 | async-start | bytes 524288 | tf_op jit(solution)/shard_map/all_to_all | solution.py:23
  261.2 1.7 fusion.52
  264.8 13.7 %all-to-all-done.7 = bf16[512,1,128]{2,1,0:T(2,128)(2,1)S(1)} async-done(((bf16[512,1,128]{2,1,0:T(2,128)(2,1)}), bf16[512,1,128]{2,1,0:T(2,128)(2,1)S(1)}, u32[]{:S(2)}, u32[]{:S(2)}) %all-to-all-start.7) | async-done | bytes 131104 | tf_op jit(solution)/shard_map/all_to_all | solution.py:23
  279.3 1.1 convolution_bitcast_fusion
  282.0 1.6 fusion.47
  284.6 1.8 fusion
  286.3 1.6 copy.39
  288.5 54.2 %all_to_all.93 = bf16[64,64,256]{2,1,0:T(8,128)(2,1)} all-to-all(bf16[64,64,256]{2,1,0:T(8,128)(2,1)S(1)} %broadcast_in_dim.18), channel_id=1, replica_groups=mesh['region'=8,'sub'=64] {'sub'}, dimensions={0} | all-to-all | bytes 4194304 | tf_op jit(solution)/shard_map/all_to_all | solution.py:72
  342.7 3.2 fusion.9
  (96 shorter events, 34.4 us)
Async XLA Ops:
  0.0 342.7 %copy-start = (bf16[1,64,4096]{2,1,0:T(8,128)(2,1)S(1)}, bf16[1,64,4096]{2,1,0:T(8,128)(2,1)}, u32[]{:S(2)}) copy-start(bf16[1,64,4096]{2,1,0:T(8,128)(2,1)} %param.15) | copy-start | bytes 1572868
  0.0 33.1 %copy-start.1 = (bf16[1,1,1024,1024]{3,2,1,0:T(8,128)(2,1)S(1)}, bf16[1,1,1024,1024]{3,2,1,0:T(8,128)(2,1)}, u32[]{:S(2)}) copy-start(bf16[1,1,1024,1024]{3,2,1,0:T(8,128)(2,1)} %param.10) | copy-start | bytes 6291460
  0.0 27.1 %copy-start.15 = (s32[4,512]{1,0:T(4,128)S(1)}, s32[4,512]{1,0:T(4,128)}, u32[]{:S(2)}) copy-start(s32[4,512]{1,0:T(4,128)} %param.13) | copy-start | bytes 24580
  4.9 39.5 %all-to-all-start = ((bf16[512,1,128]{2,1,0:T(2,128)(2,1)}), bf16[512,1,128]{2,1,0:T(2,128)(2,1)S(1)}, u32[]{:S(2)}, u32[]{:S(2)}) async-start(bf16[512,1,128]{2,1,0:T(2,128)(2,1)} %all_to_all.80), calls=%async_computation | async-start | bytes 524288 | tf_op jit(solution)/shard_map/all_to_all | solution.py:21
  47.5 28.7 %all-to-all-start.1 = ((bf16[512,1,128]{2,1,0:T(2,128)(2,1)}), bf16[512,1,128]{2,1,0:T(2,128)(2,1)S(1)}, u32[]{:S(2)}, u32[]{:S(2)}) async-start(bf16[512,1,128]{2,1,0:T(2,128)(2,1)} %copy.28), calls=%async_computation.1 | async-start | bytes 524288 | tf_op jit(solution)/shard_map/all_to_all | solution.py:23
  77.0 6.4 %copy-start.13 = (bf16[128,1024]{1,0:T(8,128)(2,1)S(1)}, bf16[128,1024]{1,0:T(8,128)(2,1)}, u32[]{:S(2)}) copy-start(bf16[128,1024]{1,0:T(8,128)(2,1)} %get-tuple-element.17) | copy-start | bytes 786436
  77.0 6.4 %copy-start.14 = (bf16[128,1024]{1,0:T(8,128)(2,1)S(1)}, bf16[128,1024]{1,0:T(8,128)(2,1)}, u32[]{:S(2)}) copy-start(bf16[128,1024]{1,0:T(8,128)(2,1)} %get-tuple-element.18) | copy-start | bytes 786436
  84.5 36.7 %all-to-all-start.2 = ((bf16[512,1,128]{2,1,0:T(2,128)(2,1)}), bf16[512,1,128]{2,1,0:T(2,128)(2,1)S(1)}, u32[]{:S(2)}, u32[]{:S(2)}) async-start(bf16[512,1,128]{2,1,0:T(2,128)(2,1)} %all_to_all.81), calls=%async_computation.2 | async-start | bytes 524288 | tf_op jit(solution)/shard_map/all_to_all | solution.py:21
  105.6 17.0 %copy-start.18 = (pred[512]{0:T(512)(128)(4,1)S(1)}, pred[512]{0:T(512)(128)(4,1)}, u32[]{:S(2)}) copy-start(pred[512]{0:T(512)(128)(4,1)} %compare_and_fusion.2) | copy-start | bytes 1540
  123.6 25.9 %all-to-all-start.3 = ((bf16[512,1,128]{2,1,0:T(2,128)(2,1)}), bf16[512,1,128]{2,1,0:T(2,128)(2,1)S(1)}, u32[]{:S(2)}, u32[]{:S(2)}) async-start(bf16[512,1,128]{2,1,0:T(2,128)(2,1)} %copy.31), calls=%async_computation.3 | async-start | bytes 524288 | tf_op jit(solution)/shard_map/all_to_all | solution.py:23
  133.7 1.0 copy-start.5
  151.0 4.8 %copy-start.11 = (bf16[128,1024]{1,0:T(8,128)(2,1)S(1)}, bf16[128,1024]{1,0:T(8,128)(2,1)}, u32[]{:S(2)}) copy-start(bf16[128,1024]{1,0:T(8,128)(2,1)} %get-tuple-element.15) | copy-start | bytes 786436
  151.0 4.8 %copy-start.12 = (bf16[128,1024]{1,0:T(8,128)(2,1)S(1)}, bf16[128,1024]{1,0:T(8,128)(2,1)}, u32[]{:S(2)}) copy-start(bf16[128,1024]{1,0:T(8,128)(2,1)} %get-tuple-element.16) | copy-start | bytes 786436
  156.9 27.0 %all-to-all-start.4 = ((bf16[512,1,128]{2,1,0:T(2,128)(2,1)}), bf16[512,1,128]{2,1,0:T(2,128)(2,1)}, u32[]{:S(2)}, u32[]{:S(2)}) async-start(bf16[512,1,128]{2,1,0:T(2,128)(2,1)} %all_to_all.82), calls=%async_computation.4 | async-start | bytes 524288 | tf_op jit(solution)/shard_map/all_to_all | solution.py:21
  169.7 16.5 %copy-start.16 = (pred[512]{0:T(512)(128)(4,1)S(1)}, pred[512]{0:T(512)(128)(4,1)}, u32[]{:S(2)}) copy-start(pred[512]{0:T(512)(128)(4,1)} %compare_and_fusion.1) | copy-start | bytes 1540
  187.2 26.8 %all-to-all-start.5 = ((bf16[512,1,128]{2,1,0:T(2,128)(2,1)}), bf16[512,1,128]{2,1,0:T(2,128)(2,1)S(1)}, u32[]{:S(2)}, u32[]{:S(2)}) async-start(bf16[512,1,128]{2,1,0:T(2,128)(2,1)} %copy.34), calls=%async_computation.5 | async-start | bytes 524288 | tf_op jit(solution)/shard_map/all_to_all | solution.py:23
  198.4 1.0 copy-start.4
  215.5 4.8 %copy-start.9 = (bf16[128,1024]{1,0:T(8,128)(2,1)S(1)}, bf16[128,1024]{1,0:T(8,128)(2,1)}, u32[]{:S(2)}) copy-start(bf16[128,1024]{1,0:T(8,128)(2,1)} %get-tuple-element.14) | copy-start | bytes 786436
  215.5 4.8 %copy-start.10 = (bf16[128,1024]{1,0:T(8,128)(2,1)S(1)}, bf16[128,1024]{1,0:T(8,128)(2,1)}, u32[]{:S(2)}) copy-start(bf16[128,1024]{1,0:T(8,128)(2,1)} %get-tuple-element.19) | copy-start | bytes 786436
  221.4 27.0 %all-to-all-start.6 = ((bf16[512,1,128]{2,1,0:T(2,128)(2,1)}), bf16[512,1,128]{2,1,0:T(2,128)(2,1)}, u32[]{:S(2)}, u32[]{:S(2)}) async-start(bf16[512,1,128]{2,1,0:T(2,128)(2,1)} %all_to_all.83), calls=%async_computation.6 | async-start | bytes 524288 | tf_op jit(solution)/shard_map/all_to_all | solution.py:21
  234.2 16.4 %copy-start.17 = (pred[512]{0:T(512)(128)(4,1)S(1)}, pred[512]{0:T(512)(128)(4,1)}, u32[]{:S(2)}) copy-start(pred[512]{0:T(512)(128)(4,1)} %compare_and_fusion) | copy-start | bytes 1540
  251.7 26.8 %all-to-all-start.7 = ((bf16[512,1,128]{2,1,0:T(2,128)(2,1)}), bf16[512,1,128]{2,1,0:T(2,128)(2,1)S(1)}, u32[]{:S(2)}, u32[]{:S(2)}) async-start(bf16[512,1,128]{2,1,0:T(2,128)(2,1)} %copy.37), calls=%async_computation.7 | async-start | bytes 524288 | tf_op jit(solution)/shard_map/all_to_all | solution.py:23
  262.9 1.0 copy-start.6
  284.5 3.4 copy-start.8
  286.3 1.7 copy-start.7
  288.5 54.3 %copy-start.2 = (f32[256,1024]{1,0:T(8,128)S(1)}, f32[256,1024]{1,0:T(8,128)}, u32[]{:S(2)}) copy-start(f32[256,1024]{1,0:T(8,128)} %fusion.6) | copy-start | bytes 3145732
  288.5 54.3 %copy-start.3 = (f32[256,1024]{1,0:T(8,128)S(1)}, f32[256,1024]{1,0:T(8,128)}, u32[]{:S(2)}) copy-start(f32[256,1024]{1,0:T(8,128)} %fusion.4) | copy-start | bytes 3145732

commit v2 on v0

--- a/solution.py
+++ b/solution.py
@@ -1,11 +1,57 @@
 import jax
 import jax.numpy as jnp
 from jax import lax
+from jax.experimental import pallas as pl
 from jax.sharding import PartitionSpec as P
 
 BLK = 128
 OVL_BLK = 2
 COLORS = 4
+ROW_TILE = 256
+
+
+def _update_kernel(inverse_ref, shaped_ref, widened_ref, accumulated_ref, accumulated_out, residual_out):
+    correction = jnp.dot(inverse_ref[...], shaped_ref[...], preferred_element_type=jnp.float32)
+    accumulated_out[...] = accumulated_ref[...] + correction
+    residual_out[...] = widened_ref[...] - 0.25 * correction
+
+
+def _first_kernel(inverse_ref, shaped_ref, widened_ref, accumulated_out, residual_out):
+    correction = jnp.dot(inverse_ref[...], shaped_ref[...], preferred_element_type=jnp.float32)
+    accumulated_out[...] = correction
+    residual_out[...] = widened_ref[...] - 0.25 * correction
+
+
+def local_update(inverse, shaped, widened, accumulated):
+    rows, columns = widened.shape
+    steps = rows // ROW_TILE
+    tile = pl.BlockSpec((ROW_TILE, columns), lambda i: (i, 0))
+    specs = [
+        pl.BlockSpec((ROW_TILE, rows), lambda i: (i, 0)),
+        pl.BlockSpec((rows, columns), lambda i: (0, 0)),
+        tile,
+    ]
+    operands = [inverse, shaped, widened]
+    if accumulated is None:
+        kernel = _first_kernel
+    else:
+        kernel = _update_kernel
+        specs.append(tile)
+        operands.append(accumulated)
+    out = jax.ShapeDtypeStruct((rows, columns), jnp.float32)
+    cost = pl.CostEstimate(
+        flops=2 * rows * rows * columns,
+        transcendentals=0,
+        bytes_accessed=rows * rows * 2 + rows * columns * 2 + rows * columns * 4 * len(operands),
+    )
+    return pl.pallas_call(
+        kernel,
+        out_shape=(out, out),
+        grid=(steps,),
+        in_specs=specs,
+        out_specs=(tile, tile),
+        cost_estimate=cost,
+    )(*operands)
 
 
 def rows_of(matrix, picked):
@@ -50,9 +96,7 @@
             upcoming = own_blocks[colour + 1]
             ahead = jnp.dot(rows_of(inverse, upcoming), shaped, preferred_element_type=jnp.float32)
             sent_rows = (rows_of(widened, upcoming) - 0.25 * ahead).astype(jnp.bfloat16)
-        correction = jnp.dot(inverse, shaped, preferred_element_type=jnp.float32)
-        accumulated = correction if accumulated is None else accumulated + correction
-        residual = widened - 0.25 * correction
+        accumulated, residual = local_update(inverse, shaped, widened, accumulated)
     settled = residual.astype(jnp.bfloat16)
     own_restriction = restriction[0, 0]
     projected = jnp.dot(own_restriction, settled, preferred_element_type=jnp.float32).astype(

time: 339 us -> 326 us (0.962)
  Pallas kernels: 0 us -> 19.6 us
  matrix products: 24.6 us -> 6.95 us
  waiting for transfers between devices: 102 us -> 118 us
  local copies, waits for them, and re-layouts: 33.7 us -> 20.6 us
  other arithmetic: 28.7 us -> 18 us
  starting transfers between devices: 88.4 us -> 82.1 us
    pallas_call x0 -> x4, Pallas kernels: none -> 19.6 us  [local_update(): pl.pallas_call(kernel, out_shape=(out, out), grid=(steps,), in_specs=spec...]
    all_to_all x4, waiting for transfers between devices: 43.6 us -> 62.4 us  [exchange(): relayed = lax.all_to_all(pieces, ('region', 'sub'), 0, 0, tiled=True)]
    dot_general x4 -> x0, matrix products: 11.9 us -> none  [shards(): correction = jnp.dot(inverse, shaped, preferred_element_type=jnp.float32)]
    dot_general x4 -> x0, local copies, waits for them, and re-layouts: 9.3 us -> none  [shards(): correction = jnp.dot(inverse, shaped, preferred_element_type=jnp.float32)]
    sub x3 -> x0, other arithmetic: 8.01 us -> none  [shards(): residual = widened - 0.25 * correction]
    convert_element_type x0 -> x4, other arithmetic: none -> 4.68 us  [shards(): shaped = widened.astype(jnp.bfloat16)]
    dot_general x3, matrix products: 4.86 us -> 0.91 us  [shards(): jnp.dot(rows_of(inverse, upcoming), shaped, preferred_element_type=jnp.fl...]
    all_to_all x4, waiting for transfers between devices: 58.8 us -> 55.2 us  [exchange(): returned = lax.all_to_all(relayed, ('region', 'sub'), 0, 0, tiled=True)]
  transfers between devices with their start and end apart: 8 -> 8, of which waited for: 8 -> 8; matrix products, arithmetic and copies ran while one was open for 9% -> 1% of each run, Pallas kernels for 0% -> 5%
where the time goes in v2:
time: 326 us; the launch traced here: 324 us
  waiting for transfers between devices  118 us (36%)
  starting transfers between devices  82.1 us (25%)
  blocking collectives  53.4 us (16%)
  local copies, waits for them, and re-layouts  20.6 us (6%)
  Pallas kernels  19.6 us (6%)
  other arithmetic  18 us (6%)
  matrix products  6.95 us (2%)
  between operations  5.62 us (2%)
    all_to_all x4, waiting for transfers between devices, exchange(): relayed = lax.all_to_all(pieces, ('region', 'sub'), 0, 0, tiled=True)  62.4 us
    all_to_all x4, waiting for transfers between devices, exchange(): returned = lax.all_to_all(relayed, ('region', 'sub'), 0, 0, tiled=True)  55.2 us
    all_to_all x1, blocking collectives, shards(): lax.all_to_all(copies, 'sub', 0, 0, tiled=True).reshape(-1, columns)  53.4 us
    all_to_all x4, starting transfers between devices, exchange(): relayed = lax.all_to_all(pieces, ('region', 'sub'), 0, 0, tiled=True)  47.4 us
    all_to_all x4, starting transfers between devices, exchange(): returned = lax.all_to_all(relayed, ('region', 'sub'), 0, 0, tiled=True)  34.7 us
    pallas_call x4, Pallas kernels, local_update(): pl.pallas_call(kernel, out_shape=(out, out), grid=(steps,), in_specs=spec...  19.6 us
    dynamic_update_slice x8, other arithmetic, shards(): lax.dynamic_update_slice_in_dim(widened, block + coupled[k * BLK:(k + 1)...  9.52 us
  transfers between devices with their start and end apart: 8, of which 8 were waited for; matrix products, arithmetic and copies ran while one was open for 1% of the time, Pallas kernels for 5%

profile of v2, /device:TPU:1, one launch (start us, length us, event | category | flops | bytes accessed | tf_op | source)
XLA Modules:
  0.0 324.0 jit_solution(9879986791998083724)
XLA Ops:
  0.0 1.6 fusion.45
  2.9 0.9 dynamic-slice_bitcast_fusion.7
  4.6 22.1 %all-to-all-start = ((bf16[512,1,128]{2,1,0:T(2,128)(2,1)}), bf16[512,1,128]{2,1,0:T(2,128)(2,1)S(1)}, u32[]{:S(2)}, u32[]{:S(2)}) async-start(bf16[512,1,128]{2,1,0:T(2,128)(2,1)} %all_to_all.80), calls=%async_computation | async-start | bytes 524288 | tf_op jit(solution)/shard_map/all_to_all | solution.py:67
  30.5 0.9 fusion.44
  31.4 2.6 dynamic-slice_bitcast_fusion.1
  34.0 10.1 %all-to-all-done = bf16[512,1,128]{2,1,0:T(2,128)(2,1)S(1)} async-done(((bf16[512,1,128]{2,1,0:T(2,128)(2,1)}), bf16[512,1,128]{2,1,0:T(2,128)(2,1)S(1)}, u32[]{:S(2)}, u32[]{:S(2)}) %all-to-all-start) | async-done | bytes 131104 | tf_op jit(solution)/shard_map/all_to_all | solution.py:67
  44.1 1.3 gather_fusion
  45.6 0.9 copy.20
  46.5 9.3 %all-to-all-start.1 = ((bf16[512,1,128]{2,1,0:T(2,128)(2,1)}), bf16[512,1,128]{2,1,0:T(2,128)(2,1)S(1)}, u32[]{:S(2)}, u32[]{:S(2)}) async-start(bf16[512,1,128]{2,1,0:T(2,128)(2,1)} %copy.20), calls=%async_computation.1 | async-start | bytes 524288 | tf_op jit(solution)/shard_map/all_to_all | solution.py:69
  56.0 17.2 %all-to-all-done.1 = bf16[512,1,128]{2,1,0:T(2,128)(2,1)S(1)} async-done(((bf16[512,1,128]{2,1,0:T(2,128)(2,1)}), bf16[512,1,128]{2,1,0:T(2,128)(2,1)S(1)}, u32[]{:S(2)}, u32[]{:S(2)}) %all-to-all-start.1) | async-done | bytes 131104 | tf_op jit(solution)/shard_map/all_to_all | solution.py:69
  74.0 1.1 convolution_bitcast_fusion.4
  75.6 0.8 all_to_all.81
  76.4 8.4 %all-to-all-start.2 = ((bf16[512,1,128]{2,1,0:T(2,128)(2,1)}), bf16[512,1,128]{2,1,0:T(2,128)(2,1)S(1)}, u32[]{:S(2)}, u32[]{:S(2)}) async-start(bf16[512,1,128]{2,1,0:T(2,128)(2,1)} %all_to_all.81), calls=%async_computation.2 | async-start | bytes 524288 | tf_op jit(solution)/shard_map/all_to_all | solution.py:67
  84.8 17.4 %all-to-all-done.2 = bf16[512,1,128]{2,1,0:T(2,128)(2,1)S(1)} async-done(((bf16[512,1,128]{2,1,0:T(2,128)(2,1)}), bf16[512,1,128]{2,1,0:T(2,128)(2,1)S(1)}, u32[]{:S(2)}, u32[]{:S(2)}) %all-to-all-start.2) | async-done | bytes 131104 | tf_op jit(solution)/shard_map/all_to_all | solution.py:67
  102.2 1.3 gather_fusion.1
  103.7 0.9 copy.22
  104.6 8.6 %all-to-all-start.3 = ((bf16[512,1,128]{2,1,0:T(2,128)(2,1)}), bf16[512,1,128]{2,1,0:T(2,128)(2,1)S(1)}, u32[]{:S(2)}, u32[]{:S(2)}) async-start(bf16[512,1,128]{2,1,0:T(2,128)(2,1)} %copy.22), calls=%async_computation.3 | async-start | bytes 524288 | tf_op jit(solution)/shard_map/all_to_all | solution.py:69
  113.3 4.7 %shard_map.73 = (f32[1024,256]{1,0:T(8,128)}, f32[1024,256]{1,0:T(8,128)}) custom-call(bf16[1024,1024]{1,0:T(8,128)(2,1)} %bitcast.103, bf16[1024,256]{1,0:T(8,128)(2,1)} %copy-done.4, f32[1024,256]{1,0:T(8,128)} %copy-done.1), custom_call_target="tpu_custom_call" | custom-call | flops 536870912 | bytes 5767168 | tf_op jit(solution)/shard_map/pallas_call | solution.py:47
  118.1 12.8 %all-to-all-done.3 = bf16[512,1,128]{2,1,0:T(2,128)(2,1)S(1)} async-done(((bf16[512,1,128]{2,1,0:T(2,128)(2,1)}), bf16[512,1,128]{2,1,0:T(2,128)(2,1)S(1)}, u32[]{:S(2)}, u32[]{:S(2)}) %all-to-all-start.3) | async-done | bytes 131104 | tf_op jit(solution)/shard_map/all_to_all | solution.py:69
  131.8 1.6 fusion.27
  133.4 1.6 fusion.26.widened_ref
  135.0 1.0 constant_dynamic-slice_fusion.2
  136.0 1.3 convert_element_type.47.shaped_ref
  138.4 8.4 %all-to-all-start.4 = ((bf16[512,1,128]{2,1,0:T(2,128)(2,1)}), bf16[512,1,128]{2,1,0:T(2,128)(2,1)S(1)}, u32[]{:S(2)}, u32[]{:S(2)}) async-start(bf16[512,1,128]{2,1,0:T(2,128)(2,1)} %all_to_all.82), calls=%async_computation.4 | async-start | bytes 524288 | tf_op jit(solution)/shard_map/all_to_all | solution.py:67
  146.8 17.5 %all-to-all-done.4 = bf16[512,1,128]{2,1,0:T(2,128)(2,1)S(1)} async-done(((bf16[512,1,128]{2,1,0:T(2,128)(2,1)}), bf16[512,1,128]{2,1,0:T(2,128)(2,1)S(1)}, u32[]{:S(2)}, u32[]{:S(2)}) %all-to-all-start.4) | async-done | bytes 131104 | tf_op jit(solution)/shard_map/all_to_all | solution.py:67
  164.3 1.3 gather_fusion.2
  165.8 0.9 copy.24
  166.8 8.4 %all-to-all-start.5 = ((bf16[512,1,128]{2,1,0:T(2,128)(2,1)}), bf16[512,1,128]{2,1,0:T(2,128)(2,1)S(1)}, u32[]{:S(2)}, u32[]{:S(2)}) async-start(bf16[512,1,128]{2,1,0:T(2,128)(2,1)} %copy.24), calls=%async_computation.5 | async-start | bytes 524288 | tf_op jit(solution)/shard_map/all_to_all | solution.py:69
  175.1 5.0 %shard_map.74 = (f32[1024,256]{1,0:T(8,128)}, f32[1024,256]{1,0:T(8,128)}) custom-call(bf16[1024,1024]{1,0:T(8,128)(2,1)} %bitcast.104, bf16[1024,256]{1,0:T(8,128)(2,1)} %copy-done.2, f32[1024,256]{1,0:T(8,128)} %fusion.26.widened_ref, f32[1024,256]{1,0:T(8,128)} %get-tuple-element.15.accumulated_ref), custom_call_target="tpu_custom_call" | custom-call | flops 536870912 | bytes 6815744 | tf_op jit(solution)/shard_map/pallas_call | solution.py:47
  180.1 12.6 %all-to-all-done.5 = bf16[512,1,128]{2,1,0:T(2,128)(2,1)S(1)} async-done(((bf16[512,1,128]{2,1,0:T(2,128)(2,1)}), bf16[512,1,128]{2,1,0:T(2,128)(2,1)S(1)}, u32[]{:S(2)}, u32[]{:S(2)}) %all-to-all-start.5) | async-done | bytes 131104 | tf_op jit(solution)/shard_map/all_to_all | solution.py:69
  193.7 1.6 fusion.25
  195.3 1.6 fusion.24.widened_ref
  196.9 1.0 constant_dynamic-slice_fusion
  197.9 1.3 convert_element_type.49.shaped_ref
  200.3 8.6 %all-to-all-start.6 = ((bf16[512,1,128]{2,1,0:T(2,128)(2,1)}), bf16[512,1,128]{2,1,0:T(2,128)(2,1)S(1)}, u32[]{:S(2)}, u32[]{:S(2)}) async-start(bf16[512,1,128]{2,1,0:T(2,128)(2,1)} %all_to_all.83), calls=%async_computation.6 | async-start | bytes 524288 | tf_op jit(solution)/shard_map/all_to_all | solution.py:67
  208.9 17.4 %all-to-all-done.6 = bf16[512,1,128]{2,1,0:T(2,128)(2,1)S(1)} async-done(((bf16[512,1,128]{2,1,0:T(2,128)(2,1)}), bf16[512,1,128]{2,1,0:T(2,128)(2,1)S(1)}, u32[]{:S(2)}, u32[]{:S(2)}) %all-to-all-start.6) | async-done | bytes 131104 | tf_op jit(solution)/shard_map/all_to_all | solution.py:67
  226.3 1.3 gather_fusion.3
  227.8 0.9 copy.26
  228.7 8.4 %all-to-all-start.7 = ((bf16[512,1,128]{2,1,0:T(2,128)(2,1)}), bf16[512,1,128]{2,1,0:T(2,128)(2,1)S(1)}, u32[]{:S(2)}, u32[]{:S(2)}) async-start(bf16[512,1,128]{2,1,0:T(2,128)(2,1)} %copy.26), calls=%async_computation.7 | async-start | bytes 524288 | tf_op jit(solution)/shard_map/all_to_all | solution.py:69
  237.1 5.0 %shard_map.75 = (f32[1024,256]{1,0:T(8,128)}, f32[1024,256]{1,0:T(8,128)}) custom-call(bf16[1024,1024]{1,0:T(8,128)(2,1)} %bitcast.105, bf16[1024,256]{1,0:T(8,128)(2,1)} %copy-done.3, f32[1024,256]{1,0:T(8,128)} %fusion.24.widened_ref, f32[1024,256]{1,0:T(8,128)} %get-tuple-element.17.accumulated_ref), custom_call_target="tpu_custom_call" | custom-call | flops 536870912 | bytes 6815744 | tf_op jit(solution)/shard_map/pallas_call | solution.py:47
  242.1 12.6 %all-to-all-done.7 = bf16[512,1,128]{2,1,0:T(2,128)(2,1)S(1)} async-done(((bf16[512,1,128]{2,1,0:T(2,128)(2,1)}), bf16[512,1,128]{2,1,0:T(2,128)(2,1)S(1)}, u32[]{:S(2)}, u32[]{:S(2)}) %all-to-all-start.7) | async-done | bytes 131104 | tf_op jit(solution)/shard_map/all_to_all | solution.py:69
  255.7 1.6 fusion.23
  257.3 1.6 fusion.22.widened_ref
  258.8 2.1 convert_element_type.51.shaped_ref
  260.9 5.0 %shard_map.76 = (f32[1024,256]{1,0:T(8,128)}, f32[1024,256]{1,0:T(8,128)}) custom-call(bf16[1024,1024]{1,0:T(8,128)(2,1)} %bitcast.106, bf16[1024,256]{1,0:T(8,128)(2,1)} %convert_element_type.51.shaped_ref, f32[1024,256]{1,0:T(8,128)} %fusion.22.widened_ref, f32[1024,256]{1,0:T(8,128)} %get-tuple-element.19.accumulated_ref), custom_call_target="tpu_custom_call" | custom-call | flops 536870912 | bytes 6815744 | tf_op jit(solution)/shard_map/pallas_call | solution.py:47
  265.9 1.4 fusion.9
  267.6 53.4 %all_to_all.93 = bf16[64,64,256]{2,1,0:T(8,128)(2,1)S(1)} all-to-all(bf16[64,64,256]{2,1,0:T(8,128)(2,1)S(1)} %broadcast_in_dim.18), channel_id=1, replica_groups=mesh['region'=8,'sub'=64] {'sub'}, dimensions={0} | all-to-all | bytes 4194304 | tf_op jit(solution)/shard_map/all_to_all | solution.py:106
  321.0 3.0 fusion.2
  (72 shorter events, 8.3 us)
Async XLA Ops:
  0.0 321.0 %copy-start = (bf16[1,64,4096]{2,1,0:T(8,128)(2,1)S(1)}, bf16[1,64,4096]{2,1,0:T(8,128)(2,1)}, u32[]{:S(2)}) copy-start(bf16[1,64,4096]{2,1,0:T(8,128)(2,1)} %param.15) | copy-start | bytes 1572868
  4.6 39.5 %all-to-all-start = ((bf16[512,1,128]{2,1,0:T(2,128)(2,1)}), bf16[512,1,128]{2,1,0:T(2,128)(2,1)S(1)}, u32[]{:S(2)}, u32[]{:S(2)}) async-start(bf16[512,1,128]{2,1,0:T(2,128)(2,1)} %all_to_all.80), calls=%async_computation | async-start | bytes 524288 | tf_op jit(solution)/shard_map/all_to_all | solution.py:67
  34.0 21.8 %copy-start.5 = (bf16[1,1,1024,256]{3,2,1,0:T(8,128)(2,1)S(1)}, bf16[1,1,1024,256]{3,2,1,0:T(8,128)(2,1)}, u32[]{:S(2)}) copy-start(bf16[1,1,1024,256]{3,2,1,0:T(8,128)(2,1)} %param.9) | copy-start | bytes 1572868
  46.5 26.6 %all-to-all-start.1 = ((bf16[512,1,128]{2,1,0:T(2,128)(2,1)}), bf16[512,1,128]{2,1,0:T(2,128)(2,1)S(1)}, u32[]{:S(2)}, u32[]{:S(2)}) async-start(bf16[512,1,128]{2,1,0:T(2,128)(2,1)} %copy.20), calls=%async_computation.1 | async-start | bytes 524288 | tf_op jit(solution)/shard_map/all_to_all | solution.py:69
  56.0 19.3 %copy-start.12 = (bf16[128,1024]{1,0:T(8,128)(2,1)S(1)}, bf16[128,1024]{1,0:T(8,128)(2,1)}, u32[]{:S(2)}) copy-start(bf16[128,1024]{1,0:T(8,128)(2,1)} %get-tuple-element.25) | copy-start | bytes 786436
  56.0 19.3 %copy-start.13 = (bf16[128,1024]{1,0:T(8,128)(2,1)S(1)}, bf16[128,1024]{1,0:T(8,128)(2,1)}, u32[]{:S(2)}) copy-start(bf16[128,1024]{1,0:T(8,128)(2,1)} %get-tuple-element.26) | copy-start | bytes 786436
  75.1 1.2 copy-start.1
  75.3 28.3 %copy-start.4 = (bf16[1024,256]{1,0:T(8,128)(2,1)}, bf16[1024,256]{1,0:T(8,128)(2,1)S(1)}, u32[]{:S(2)}) copy-start(bf16[1024,256]{1,0:T(8,128)(2,1)S(1)} %convert_element_type.45.shaped_ref) | copy-start | bytes 1572868
  76.4 25.8 %all-to-all-start.2 = ((bf16[512,1,128]{2,1,0:T(2,128)(2,1)}), bf16[512,1,128]{2,1,0:T(2,128)(2,1)S(1)}, u32[]{:S(2)}, u32[]{:S(2)}) async-start(bf16[512,1,128]{2,1,0:T(2,128)(2,1)} %all_to_all.81), calls=%async_computation.2 | async-start | bytes 524288 | tf_op jit(solution)/shard_map/all_to_all | solution.py:67
  104.6 26.2 %all-to-all-start.3 = ((bf16[512,1,128]{2,1,0:T(2,128)(2,1)}), bf16[512,1,128]{2,1,0:T(2,128)(2,1)S(1)}, u32[]{:S(2)}, u32[]{:S(2)}) async-start(bf16[512,1,128]{2,1,0:T(2,128)(2,1)} %copy.22), calls=%async_computation.3 | async-start | bytes 524288 | tf_op jit(solution)/shard_map/all_to_all | solution.py:69
  113.3 18.3 %copy-start.7 = (bf16[1,1,4,256,256]{4,3,2,1,0:T(8,128)(2,1)S(1)}, bf16[1,1,4,256,256]{4,3,2,1,0:T(8,128)(2,1)}, u32[]{:S(2)}) copy-start(bf16[1,1,4,256,256]{4,3,2,1,0:T(8,128)(2,1)} %param.11) | copy-start | bytes 1572868
  118.1 19.2 %copy-start.10 = (bf16[128,1024]{1,0:T(8,128)(2,1)S(1)}, bf16[128,1024]{1,0:T(8,128)(2,1)}, u32[]{:S(2)}) copy-start(bf16[128,1024]{1,0:T(8,128)(2,1)} %get-tuple-element.23) | copy-start | bytes 786436
  118.1 19.2 %copy-start.11 = (bf16[128,1024]{1,0:T(8,128)(2,1)S(1)}, bf16[128,1024]{1,0:T(8,128)(2,1)}, u32[]{:S(2)}) copy-start(bf16[128,1024]{1,0:T(8,128)(2,1)} %get-tuple-element.24) | copy-start | bytes 786436
  137.3 28.4 %copy-start.2 = (bf16[1024,256]{1,0:T(8,128)(2,1)}, bf16[1024,256]{1,0:T(8,128)(2,1)S(1)}, u32[]{:S(2)}) copy-start(bf16[1024,256]{1,0:T(8,128)(2,1)S(1)} %convert_element_type.47.shaped_ref) | copy-start | bytes 1572868
  138.4 25.9 %all-to-all-start.4 = ((bf16[512,1,128]{2,1,0:T(2,128)(2,1)}), bf16[512,1,128]{2,1,0:T(2,128)(2,1)S(1)}, u32[]{:S(2)}, u32[]{:S(2)}) async-start(bf16[512,1,128]{2,1,0:T(2,128)(2,1)} %all_to_all.82), calls=%async_computation.4 | async-start | bytes 524288 | tf_op jit(solution)/shard_map/all_to_all | solution.py:67
  166.8 26.0 %all-to-all-start.5 = ((bf16[512,1,128]{2,1,0:T(2,128)(2,1)}), bf16[512,1,128]{2,1,0:T(2,128)(2,1)S(1)}, u32[]{:S(2)}, u32[]{:S(2)}) async-start(bf16[512,1,128]{2,1,0:T(2,128)(2,1)} %copy.24), calls=%async_computation.5 | async-start | bytes 524288 | tf_op jit(solution)/shard_map/all_to_all | solution.py:69
  180.1 19.1 %copy-start.8 = (bf16[128,1024]{1,0:T(8,128)(2,1)S(1)}, bf16[128,1024]{1,0:T(8,128)(2,1)}, u32[]{:S(2)}) copy-start(bf16[128,1024]{1,0:T(8,128)(2,1)} %get-tuple-element.22) | copy-start | bytes 786436
  180.1 19.1 %copy-start.9 = (bf16[128,1024]{1,0:T(8,128)(2,1)S(1)}, bf16[128,1024]{1,0:T(8,128)(2,1)}, u32[]{:S(2)}) copy-start(bf16[128,1024]{1,0:T(8,128)(2,1)} %get-tuple-element.27) | copy-start | bytes 786436
  199.2 28.5 %copy-start.3 = (bf16[1024,256]{1,0:T(8,128)(2,1)}, bf16[1024,256]{1,0:T(8,128)(2,1)S(1)}, u32[]{:S(2)}) copy-start(bf16[1024,256]{1,0:T(8,128)(2,1)S(1)} %convert_element_type.49.shaped_ref) | copy-start | bytes 1572868
  200.3 26.0 %all-to-all-start.6 = ((bf16[512,1,128]{2,1,0:T(2,128)(2,1)}), bf16[512,1,128]{2,1,0:T(2,128)(2,1)S(1)}, u32[]{:S(2)}, u32[]{:S(2)}) async-start(bf16[512,1,128]{2,1,0:T(2,128)(2,1)} %all_to_all.83), calls=%async_computation.6 | async-start | bytes 524288 | tf_op jit(solution)/shard_map/all_to_all | solution.py:67
  228.7 26.0 %all-to-all-start.7 = ((bf16[512,1,128]{2,1,0:T(2,128)(2,1)}), bf16[512,1,128]{2,1,0:T(2,128)(2,1)S(1)}, u32[]{:S(2)}, u32[]{:S(2)}) async-start(bf16[512,1,128]{2,1,0:T(2,128)(2,1)} %copy.26), calls=%async_computation.7 | async-start | bytes 524288 | tf_op jit(solution)/shard_map/all_to_all | solution.py:69
  260.9 5.0 %copy-start.6 = (bf16[1,1,64,1024]{3,2,1,0:T(8,128)(2,1)S(1)}, bf16[1,1,64,1024]{3,2,1,0:T(8,128)(2,1)}, u32[]{:S(2)}) copy-start(bf16[1,1,64,1024]{3,2,1,0:T(8,128)(2,1)} %param.14) | copy-start | bytes 393220

commit v3 on v1

--- a/solution.py
+++ b/solution.py
@@ -1,11 +1,69 @@
 import jax
 import jax.numpy as jnp
 from jax import lax
+from jax.experimental import pallas as pl
+from jax.experimental.pallas import tpu as pltpu
 from jax.sharding import PartitionSpec as P
 
 BLK = 128
 OVL_BLK = 2
 COLORS = 4
+
+
+def _update_body(picked_ref, inverse_ref, shaped_ref, residual_ref, coupled_ref, accumulated_ref, accumulated_out, residual_out, base_out):
+    block = pl.program_id(0)
+    correction = jnp.dot(inverse_ref[...], shaped_ref[...], preferred_element_type=jnp.float32)
+    widened = residual_ref[...]
+    for k in range(OVL_BLK):
+        widened = jnp.where(picked_ref[k] == block, widened + coupled_ref[k * BLK:(k + 1) * BLK, :], widened)
+    if accumulated_ref is None:
+        accumulated_out[...] = correction
+    else:
+        accumulated_out[...] = accumulated_ref[...] + correction
+    updated = widened - 0.25 * correction
+    residual_out[...] = updated
+    base_out[...] = updated.astype(jnp.bfloat16)
+
+
+def _first_kernel(picked_ref, inverse_ref, shaped_ref, residual_ref, coupled_ref, accumulated_out, residual_out, base_out):
+    _update_body(picked_ref, inverse_ref, shaped_ref, residual_ref, coupled_ref, None, accumulated_out, residual_out, base_out)
+
+
+def local_update(picked, inverse, shaped, residual, coupled, accumulated):
+    rows, columns = residual.shape
+    tile = pl.BlockSpec((BLK, columns), lambda i, p: (i, 0))
+    specs = [
+        pl.BlockSpec((BLK, rows), lambda i, p: (i, 0)),
+        pl.BlockSpec((rows, columns), lambda i, p: (0, 0)),
+        tile,
+        pl.BlockSpec(coupled.shape, lambda i, p: (0, 0)),
+    ]
+    operands = [inverse, shaped, residual, coupled]
+    if accumulated is None:
+        kernel = _first_kernel
+    else:
+        kernel = _update_body
+        specs.append(tile)
+        operands.append(accumulated)
+    wide = jax.ShapeDtypeStruct((rows, columns), jnp.float32)
+    narrow = jax.ShapeDtypeStruct((rows, columns), jnp.bfloat16)
+    cost = pl.CostEstimate(
+        flops=2 * rows * rows * columns,
+        transcendentals=0,
+        bytes_accessed=rows * rows * 2 + rows * columns * (2 + 4 * len(operands) + 2),
+    )
+    grid_spec = pltpu.PrefetchScalarGridSpec(
+        num_scalar_prefetch=1,
+        grid=(rows // BLK,),
+        in_specs=specs,
+        out_specs=(tile, tile, tile),
+    )
+    return pl.pallas_call(
+        kernel,
+        out_shape=(wide, wide, narrow),
+        grid_spec=grid_spec,
+        cost_estimate=cost,
+    )(picked, *operands)
 
 
 def rows_of(matrix, picked):
@@ -31,27 +89,25 @@
     columns = right_side.shape[-1]
     sub_peers = lax.axis_size("sub")
     all_peers = sub_peers * lax.axis_size("region")
-    residual = right_side[0, 0].astype(jnp.float32)
+    base = right_side[0, 0]
+    residual = base.astype(jnp.float32)
     accumulated = None
-    sent_rows = rows_of(right_side[0, 0], own_blocks[0])
+    sent_rows = rows_of(base, own_blocks[0])
     for colour in range(COLORS):
         picked = own_blocks[colour]
         received = exchange(sent_rows, partner[colour], all_peers)
-        base = residual.astype(jnp.bfloat16)
         if colour + 1 < COLORS:
-            next_inverse_rows = rows_of(inverse, own_blocks[colour + 1])
-            next_residual_rows = rows_of(residual, own_blocks[colour + 1])
+            upcoming = own_blocks[colour + 1]
+            next_inverse_rows = rows_of(inverse, upcoming)
+            next_residual_rows = rows_of(residual, upcoming)
         coupled = jnp.dot(tile_set[colour], received, preferred_element_type=jnp.float32)
         parts = [coupled[k * BLK:(k + 1) * BLK] for k in range(OVL_BLK)]
-        widened = residual
         shaped = base
         for k in range(OVL_BLK):
             start = picked[k] * BLK
             block = lax.dynamic_slice_in_dim(residual, start, BLK, axis=0) + parts[k]
-            widened = lax.dynamic_update_slice_in_dim(widened, block, start, axis=0)
             shaped = lax.dynamic_update_slice_in_dim(shaped, block.astype(jnp.bfloat16), start, axis=0)
         if colour + 1 < COLORS:
-            upcoming = own_blocks[colour + 1]
             ahead = jnp.dot(next_inverse_rows, shaped, preferred_element_type=jnp.float32)
             near = []
             for j in range(OVL_BLK):
@@ -60,12 +116,9 @@
                     row = jnp.where(upcoming[j] == picked[k], row + parts[k], row)
                 near.append(row)
             sent_rows = (jnp.concatenate(near, axis=0) - 0.25 * ahead).astype(jnp.bfloat16)
-        correction = jnp.dot(inverse, shaped, preferred_element_type=jnp.float32)
-        accumulated = correction if accumulated is None else accumulated + correction
-        residual = widened - 0.25 * correction
-    settled = residual.astype(jnp.bfloat16)
+        accumulated, residual, base = local_update(picked, inverse, shaped, residual, coupled, accumulated)
     own_restriction = restriction[0, 0]
-    projected = jnp.dot(own_restriction, settled, preferred_element_type=jnp.float32).astype(
+    projected = jnp.dot(own_restriction, base, preferred_element_type=jnp.float32).astype(
         jnp.bfloat16
     )
     copies = jnp.broadcast_to(projected[None], (sub_peers,) + projected.shape)

time: 349 us -> 333 us (0.954)
  Pallas kernels: 0 us -> 31.7 us
  local copies, waits for them, and re-layouts: 38.9 us -> 17.5 us
  other arithmetic: 33.1 us -> 15.4 us
  starting transfers between devices: 101 us -> 88.1 us
  waiting for transfers between devices: 83.3 us -> 95 us
  matrix products: 16 us -> 9.04 us
    pallas_call x0 -> x4, Pallas kernels: none -> 31.7 us  [local_update(): pl.pallas_call(kernel, out_shape=(wide, wide, narrow), grid_spec=grid_spe...]
    all_to_all x4, starting transfers between devices: 63.6 us -> 50 us  [exchange(): relayed = lax.all_to_all(pieces, ('region', 'sub'), 0, 0, tiled=True)]
    unnamed x47 -> x39, local copies, waits for them, and re-layouts: 11.3 us -> 1.34 us
    dot_general x4 -> x0, local copies, waits for them, and re-layouts: 9.35 us -> none  [shards(): correction = jnp.dot(inverse, shaped, preferred_element_type=jnp.float32)]
    all_to_all x4, waiting for transfers between devices: 42.1 us -> 48.7 us  [exchange(): relayed = lax.all_to_all(pieces, ('region', 'sub'), 0, 0, tiled=True)]
    dynamic_update_slice x4 -> x0, other arithmetic: 6.3 us -> none  [shards(): widened = lax.dynamic_update_slice_in_dim(widened, block, start, axis=0)]
    convert_element_type x4 -> x1, other arithmetic: 6.25 us -> 0.07 us  [shards(): residual = base.astype(jnp.float32)]
    dot_general x5 -> x1, matrix products: 7.3 us -> 1.25 us  [shards(): jnp.dot(own_restriction, base, preferred_element_type=jnp.float32)]
  transfers between devices with their start and end apart: 8 -> 8, of which waited for: 7 -> 8; matrix products, arithmetic and copies ran while one was open for 9% -> 1% of each run, Pallas kernels for 0% -> 7%
where the time goes in v3:
time: 333 us; the launch traced here: 331 us
  waiting for transfers between devices  95 us (29%)
  starting transfers between devices  88.1 us (26%)
  blocking collectives  53.4 us (16%)
  Pallas kernels  31.7 us (10%)
  between operations  20.6 us (6%)
  local copies, waits for them, and re-layouts  17.5 us (5%)
  other arithmetic  15.4 us (5%)
  matrix products  9.04 us (3%)
    all_to_all x1, blocking collectives, shards(): lax.all_to_all(copies, 'sub', 0, 0, tiled=True).reshape(-1, columns)  53.4 us
    all_to_all x4, starting transfers between devices, exchange(): relayed = lax.all_to_all(pieces, ('region', 'sub'), 0, 0, tiled=True)  50 us
    all_to_all x4, waiting for transfers between devices, exchange(): relayed = lax.all_to_all(pieces, ('region', 'sub'), 0, 0, tiled=True)  48.7 us
    all_to_all x4, waiting for transfers between devices, exchange(): returned = lax.all_to_all(relayed, ('region', 'sub'), 0, 0, tiled=True)  46.3 us
    all_to_all x4, starting transfers between devices, exchange(): returned = lax.all_to_all(relayed, ('region', 'sub'), 0, 0, tiled=True)  38.1 us
    pallas_call x4, Pallas kernels, local_update(): pl.pallas_call(kernel, out_shape=(wide, wide, narrow), grid_spec=grid_spe...  31.7 us
    dynamic_update_slice x8, other arithmetic, shards(): lax.dynamic_update_slice_in_dim(shaped, block.astype(jnp.bfloat16), start...  9.6 us
  transfers between devices with their start and end apart: 8, of which 8 were waited for; matrix products, arithmetic and copies ran while one was open for 1% of the time, Pallas kernels for 7%

profile of v3, /device:TPU:1, one launch (start us, length us, event | category | flops | bytes accessed | tf_op | source)
XLA Modules:
  0.0 330.9 jit_solution(12418332975336456907)
XLA Ops:
  0.0 1.2 copy.52
  1.2 1.7 fusion.45
  4.9 22.1 %all-to-all-start = ((bf16[512,1,128]{2,1,0:T(2,128)(2,1)}), bf16[512,1,128]{2,1,0:T(2,128)(2,1)S(1)}, u32[]{:S(2)}, u32[]{:S(2)}) async-start(bf16[512,1,128]{2,1,0:T(2,128)(2,1)} %all_to_all.80), calls=%async_computation | async-start | bytes 524288 | tf_op jit(solution)/shard_map/all_to_all | solution.py:79
  27.1 0.8 slice_reduce_fusion
  31.8 1.2 dynamic-slice_bitcast_fusion.1
  37.9 6.5 %all-to-all-done = bf16[512,1,128]{2,1,0:T(2,128)(2,1)S(1)} async-done(((bf16[512,1,128]{2,1,0:T(2,128)(2,1)}), bf16[512,1,128]{2,1,0:T(2,128)(2,1)S(1)}, u32[]{:S(2)}, u32[]{:S(2)}) %all-to-all-start) | async-done | bytes 131104 | tf_op jit(solution)/shard_map/all_to_all | solution.py:79
  44.4 1.3 gather_fusion
  45.9 0.9 copy.20
  46.8 12.9 %all-to-all-start.1 = ((bf16[512,1,128]{2,1,0:T(2,128)(2,1)}), bf16[512,1,128]{2,1,0:T(2,128)(2,1)S(1)}, u32[]{:S(2)}, u32[]{:S(2)}) async-start(bf16[512,1,128]{2,1,0:T(2,128)(2,1)} %copy.20), calls=%async_computation.1 | async-start | bytes 524288 | tf_op jit(solution)/shard_map/all_to_all | solution.py:81
  59.8 17.3 %all-to-all-done.1 = bf16[512,1,128]{2,1,0:T(2,128)(2,1)S(1)} async-done(((bf16[512,1,128]{2,1,0:T(2,128)(2,1)}), bf16[512,1,128]{2,1,0:T(2,128)(2,1)S(1)}, u32[]{:S(2)}, u32[]{:S(2)}) %all-to-all-start.1) | async-done | bytes 131104 | tf_op jit(solution)/shard_map/all_to_all | solution.py:81
  77.1 0.8 reduce.4
  78.3 1.4 fusion.8
  80.4 8.3 %all-to-all-start.2 = ((bf16[512,1,128]{2,1,0:T(2,128)(2,1)}), bf16[512,1,128]{2,1,0:T(2,128)(2,1)S(1)}, u32[]{:S(2)}, u32[]{:S(2)}) async-start(bf16[512,1,128]{2,1,0:T(2,128)(2,1)} %all_to_all.81), calls=%async_computation.2 | async-start | bytes 524288 | tf_op jit(solution)/shard_map/all_to_all | solution.py:79
  93.8 12.5 %all-to-all-done.2 = bf16[512,1,128]{2,1,0:T(2,128)(2,1)S(1)} async-done(((bf16[512,1,128]{2,1,0:T(2,128)(2,1)}), bf16[512,1,128]{2,1,0:T(2,128)(2,1)S(1)}, u32[]{:S(2)}, u32[]{:S(2)}) %all-to-all-start.2) | async-done | bytes 131104 | tf_op jit(solution)/shard_map/all_to_all | solution.py:79
  106.4 1.3 gather_fusion.1
  107.9 0.9 copy.22
  108.8 8.5 %all-to-all-start.3 = ((bf16[512,1,128]{2,1,0:T(2,128)(2,1)}), bf16[512,1,128]{2,1,0:T(2,128)(2,1)S(1)}, u32[]{:S(2)}, u32[]{:S(2)}) async-start(bf16[512,1,128]{2,1,0:T(2,128)(2,1)} %copy.22), calls=%async_computation.3 | async-start | bytes 524288 | tf_op jit(solution)/shard_map/all_to_all | solution.py:81
  117.3 7.6 %shard_map.73 = (f32[1024,256]{1,0:T(8,128)}, f32[1024,256]{1,0:T(8,128)}, bf16[1024,256]{1,0:T(8,128)(2,1)}) custom-call(s32[2]{0:T(128)} %get-tuple-element.28.picked_ref, bf16[1024,1024]{1,0:T(8,128)(2,1)} %bitcast.114, bf16[1024,256]{1,0:T(8,128)(2,1)} %copy-done.3, f32[1024,256]{1,0:T(8,128)} %copy-done.2, f32[256,256]{1,0:T(8,128)} %copy-done.5), custom_call_target="tpu_custom_call" | custom-call | flops 536870912 | bytes 7340032 | tf_op jit(solution)/shard_map/pallas_call | solution.py:61
  125.0 9.9 %all-to-all-done.3 = bf16[512,1,128]{2,1,0:T(2,128)(2,1)S(1)} async-done(((bf16[512,1,128]{2,1,0:T(2,128)(2,1)}), bf16[512,1,128]{2,1,0:T(2,128)(2,1)S(1)}, u32[]{:S(2)}, u32[]{:S(2)}) %all-to-all-start.3) | async-done | bytes 131104 | tf_op jit(solution)/shard_map/all_to_all | solution.py:81
  135.9 1.6 fusion.35
  137.5 1.5 fusion.36.shaped_ref
  139.1 1.0 add_select_fusion.6
  140.1 1.3 fusion.7
  142.2 9.6 %all-to-all-start.4 = ((bf16[512,1,128]{2,1,0:T(2,128)(2,1)}), bf16[512,1,128]{2,1,0:T(2,128)(2,1)S(1)}, u32[]{:S(2)}, u32[]{:S(2)}) async-start(bf16[512,1,128]{2,1,0:T(2,128)(2,1)} %all_to_all.82), calls=%async_computation.4 | async-start | bytes 524288 | tf_op jit(solution)/shard_map/all_to_all | solution.py:79
  156.9 12.3 %all-to-all-done.4 = bf16[512,1,128]{2,1,0:T(2,128)(2,1)S(1)} async-done(((bf16[512,1,128]{2,1,0:T(2,128)(2,1)}), bf16[512,1,128]{2,1,0:T(2,128)(2,1)S(1)}, u32[]{:S(2)}, u32[]{:S(2)}) %all-to-all-start.4) | async-done | bytes 131104 | tf_op jit(solution)/shard_map/all_to_all | solution.py:79
  169.2 1.3 gather_fusion.2
  170.7 0.9 copy.24
  171.6 8.4 %all-to-all-start.5 = ((bf16[512,1,128]{2,1,0:T(2,128)(2,1)}), bf16[512,1,128]{2,1,0:T(2,128)(2,1)S(1)}, u32[]{:S(2)}, u32[]{:S(2)}) async-start(bf16[512,1,128]{2,1,0:T(2,128)(2,1)} %copy.24), calls=%async_computation.5 | async-start | bytes 524288 | tf_op jit(solution)/shard_map/all_to_all | solution.py:81
  180.0 8.0 %shard_map.74 = (f32[1024,256]{1,0:T(8,128)}, f32[1024,256]{1,0:T(8,128)}, bf16[1024,256]{1,0:T(8,128)(2,1)}) custom-call(s32[2]{0:T(128)} %get-tuple-element.29.picked_ref, bf16[1024,1024]{1,0:T(8,128)(2,1)} %bitcast.115, bf16[1024,256]{1,0:T(8,128)(2,1)} %fusion.36.shaped_ref, f32[1024,256]{1,0:T(8,128)} %get-tuple-element.18.residual_ref, ...), custom_call_target="tpu_custom_call" | custom-call | flops 536870912 | bytes 8388608 | tf_op jit(solution)/shard_map/pallas_call | solution.py:61
  188.0 9.6 %all-to-all-done.5 = bf16[512,1,128]{2,1,0:T(2,128)(2,1)S(1)} async-done(((bf16[512,1,128]{2,1,0:T(2,128)(2,1)}), bf16[512,1,128]{2,1,0:T(2,128)(2,1)S(1)}, u32[]{:S(2)}, u32[]{:S(2)}) %all-to-all-start.5) | async-done | bytes 131104 | tf_op jit(solution)/shard_map/all_to_all | solution.py:81
  198.6 1.7 fusion.37
  200.3 1.5 fusion.38.shaped_ref
  201.8 1.0 add_select_fusion.2
  202.8 1.3 fusion.6
  204.2 0.8 all_to_all.83
  205.0 9.9 %all-to-all-start.6 = ((bf16[512,1,128]{2,1,0:T(2,128)(2,1)}), bf16[512,1,128]{2,1,0:T(2,128)(2,1)S(1)}, u32[]{:S(2)}, u32[]{:S(2)}) async-start(bf16[512,1,128]{2,1,0:T(2,128)(2,1)} %all_to_all.83), calls=%async_computation.6 | async-start | bytes 524288 | tf_op jit(solution)/shard_map/all_to_all | solution.py:79
  214.9 17.4 %all-to-all-done.6 = bf16[512,1,128]{2,1,0:T(2,128)(2,1)S(1)} async-done(((bf16[512,1,128]{2,1,0:T(2,128)(2,1)}), bf16[512,1,128]{2,1,0:T(2,128)(2,1)S(1)}, u32[]{:S(2)}, u32[]{:S(2)}) %all-to-all-start.6) | async-done | bytes 131104 | tf_op jit(solution)/shard_map/all_to_all | solution.py:79
  232.3 1.3 gather_fusion.3
  233.8 0.9 copy.26
  234.7 8.3 %all-to-all-start.7 = ((bf16[512,1,128]{2,1,0:T(2,128)(2,1)}), bf16[512,1,128]{2,1,0:T(2,128)(2,1)S(1)}, u32[]{:S(2)}, u32[]{:S(2)}) async-start(bf16[512,1,128]{2,1,0:T(2,128)(2,1)} %copy.26), calls=%async_computation.7 | async-start | bytes 524288 | tf_op jit(solution)/shard_map/all_to_all | solution.py:81
  243.1 8.0 %shard_map.75 = (f32[1024,256]{1,0:T(8,128)}, f32[1024,256]{1,0:T(8,128)}, bf16[1024,256]{1,0:T(8,128)(2,1)}) custom-call(s32[2]{0:T(128)} %get-tuple-element.30.picked_ref, bf16[1024,1024]{1,0:T(8,128)(2,1)} %bitcast.116, bf16[1024,256]{1,0:T(8,128)(2,1)} %fusion.38.shaped_ref, f32[1024,256]{1,0:T(8,128)} %get-tuple-element.21.residual_ref, ...), custom_call_target="tpu_custom_call" | custom-call | flops 536870912 | bytes 8388608 | tf_op jit(solution)/shard_map/pallas_call | solution.py:61
  251.1 9.6 %all-to-all-done.7 = bf16[512,1,128]{2,1,0:T(2,128)(2,1)S(1)} async-done(((bf16[512,1,128]{2,1,0:T(2,128)(2,1)}), bf16[512,1,128]{2,1,0:T(2,128)(2,1)S(1)}, u32[]{:S(2)}, u32[]{:S(2)}) %all-to-all-start.7) | async-done | bytes 131104 | tf_op jit(solution)/shard_map/all_to_all | solution.py:81
  261.7 1.6 fusion.39
  263.3 1.5 fusion.40.shaped_ref
  264.9 8.1 %shard_map.76 = (f32[1024,256]{1,0:T(8,128)}, f32[1024,256]{1,0:T(8,128)}, bf16[1024,256]{1,0:T(8,128)(2,1)}) custom-call(s32[2]{0:T(128)} %get-tuple-element.31.picked_ref, bf16[1024,1024]{1,0:T(8,128)(2,1)} %bitcast.117, bf16[1024,256]{1,0:T(8,128)(2,1)} %fusion.40.shaped_ref, f32[1024,256]{1,0:T(8,128)} %get-tuple-element.24.residual_ref, ...), custom_call_target="tpu_custom_call" | custom-call | flops 536870912 | bytes 8388608 | tf_op jit(solution)/shard_map/pallas_call | solution.py:61
  273.0 1.2 fusion.9
  274.5 53.4 %all_to_all.93 = bf16[64,64,256]{2,1,0:T(8,128)(2,1)S(1)} all-to-all(bf16[64,64,256]{2,1,0:T(8,128)(2,1)S(1)} %broadcast_in_dim.18), channel_id=1, replica_groups=mesh['region'=8,'sub'=64] {'sub'}, dimensions={0} | all-to-all | bytes 4194304 | tf_op jit(solution)/shard_map/all_to_all | solution.py:125
  327.9 3.0 fusion.2
  (76 shorter events, 6.7 us)
Async XLA Ops:
  0.0 327.9 %copy-start = (bf16[1,64,4096]{2,1,0:T(8,128)(2,1)S(1)}, bf16[1,64,4096]{2,1,0:T(8,128)(2,1)}, u32[]{:S(2)}) copy-start(bf16[1,64,4096]{2,1,0:T(8,128)(2,1)} %param.15) | copy-start | bytes 1572868
  0.0 31.8 %copy-start.1 = (bf16[1,1,1024,1024]{3,2,1,0:T(8,128)(2,1)S(1)}, bf16[1,1,1024,1024]{3,2,1,0:T(8,128)(2,1)}, u32[]{:S(2)}) copy-start(bf16[1,1,1024,1024]{3,2,1,0:T(8,128)(2,1)} %param.10) | copy-start | bytes 6291460
  0.0 27.0 %copy-start.15 = (s32[4,1,1,2]{0,3,2,1:T(2,128)S(1)}, s32[4,1,1,2]{0,3,2,1:T(2,128)}, u32[]{:S(2)}) copy-start(s32[4,1,1,2]{0,3,2,1:T(2,128)} %param.12) | copy-start | bytes 100
  0.0 31.7 %copy-start.16 = (s32[4,512]{1,0:T(4,128)S(1)}, s32[4,512]{1,0:T(4,128)}, u32[]{:S(2)}) copy-start(s32[4,512]{1,0:T(4,128)} %param.13) | copy-start | bytes 24580
  4.9 39.5 %all-to-all-start = ((bf16[512,1,128]{2,1,0:T(2,128)(2,1)}), bf16[512,1,128]{2,1,0:T(2,128)(2,1)S(1)}, u32[]{:S(2)}, u32[]{:S(2)}) async-start(bf16[512,1,128]{2,1,0:T(2,128)(2,1)} %all_to_all.80), calls=%async_computation | async-start | bytes 524288 | tf_op jit(solution)/shard_map/all_to_all | solution.py:79
  44.4 33.5 %copy-start.9 = (bf16[1,1,4,256,256]{4,3,2,1,0:T(8,128)(2,1)S(1)}, bf16[1,1,4,256,256]{4,3,2,1,0:T(8,128)(2,1)}, u32[]{:S(2)}) copy-start(bf16[1,1,4,256,256]{4,3,2,1,0:T(8,128)(2,1)} %param.11) | copy-start | bytes 1572868
  46.8 30.2 %all-to-all-start.1 = ((bf16[512,1,128]{2,1,0:T(2,128)(2,1)}), bf16[512,1,128]{2,1,0:T(2,128)(2,1)S(1)}, u32[]{:S(2)}, u32[]{:S(2)}) async-start(bf16[512,1,128]{2,1,0:T(2,128)(2,1)} %copy.20), calls=%async_computation.1 | async-start | bytes 524288 | tf_op jit(solution)/shard_map/all_to_all | solution.py:81
  59.7 18.5 %copy-start.14 = (bf16[128,1024]{1,0:T(8,128)(2,1)S(1)}, bf16[128,1024]{1,0:T(8,128)(2,1)}, u32[]{:S(2)}) copy-start(bf16[128,1024]{1,0:T(8,128)(2,1)} %get-tuple-element.35) | copy-start | bytes 786436
  59.8 19.8 %copy-start.2 = (f32[1024,256]{1,0:T(8,128)}, f32[1024,256]{1,0:T(8,128)S(1)}, u32[]{:S(2)}) copy-start(f32[1024,256]{1,0:T(8,128)S(1)} %bitcast_convert_fusion.residual_ref) | copy-start | bytes 3145732
  78.1 2.3 copy-start.5
  78.2 29.5 %copy-start.3 = (bf16[1024,256]{1,0:T(8,128)(2,1)}, bf16[1024,256]{1,0:T(8,128)(2,1)S(1)}, u32[]{:S(2)}) copy-start(bf16[1024,256]{1,0:T(8,128)(2,1)S(1)} %fusion.34.shaped_ref) | copy-start | bytes 1572868
  80.4 25.9 %all-to-all-start.2 = ((bf16[512,1,128]{2,1,0:T(2,128)(2,1)}), bf16[512,1,128]{2,1,0:T(2,128)(2,1)S(1)}, u32[]{:S(2)}, u32[]{:S(2)}) async-start(bf16[512,1,128]{2,1,0:T(2,128)(2,1)} %all_to_all.81), calls=%async_computation.2 | async-start | bytes 524288 | tf_op jit(solution)/shard_map/all_to_all | solution.py:79
  108.8 26.1 %all-to-all-start.3 = ((bf16[512,1,128]{2,1,0:T(2,128)(2,1)}), bf16[512,1,128]{2,1,0:T(2,128)(2,1)S(1)}, u32[]{:S(2)}, u32[]{:S(2)}) async-start(bf16[512,1,128]{2,1,0:T(2,128)(2,1)} %copy.22), calls=%async_computation.3 | async-start | bytes 524288 | tf_op jit(solution)/shard_map/all_to_all | solution.py:81
  124.9 15.1 %copy-start.12 = (bf16[128,1024]{1,0:T(8,128)(2,1)S(1)}, bf16[128,1024]{1,0:T(8,128)(2,1)}, u32[]{:S(2)}) copy-start(bf16[128,1024]{1,0:T(8,128)(2,1)} %get-tuple-element.33) | copy-start | bytes 786436
  124.9 15.1 %copy-start.13 = (bf16[128,1024]{1,0:T(8,128)(2,1)S(1)}, bf16[128,1024]{1,0:T(8,128)(2,1)}, u32[]{:S(2)}) copy-start(bf16[128,1024]{1,0:T(8,128)(2,1)} %get-tuple-element.34) | copy-start | bytes 786436
  135.9 6.3 %copy-start.4 = (f32[256,256]{1,0:T(8,128)}, f32[256,256]{1,0:T(8,128)S(1)}, u32[]{:S(2)}) copy-start(f32[256,256]{1,0:T(8,128)S(1)} %convolution_bitcast_fusion.3.coupled_ref) | copy-start | bytes 786436
  142.2 27.0 %all-to-all-start.4 = ((bf16[512,1,128]{2,1,0:T(2,128)(2,1)}), bf16[512,1,128]{2,1,0:T(2,128)(2,1)S(1)}, u32[]{:S(2)}, u32[]{:S(2)}) async-start(bf16[512,1,128]{2,1,0:T(2,128)(2,1)} %all_to_all.82), calls=%async_computation.4 | async-start | bytes 524288 | tf_op jit(solution)/shard_map/all_to_all | solution.py:79
  171.6 26.0 %all-to-all-start.5 = ((bf16[512,1,128]{2,1,0:T(2,128)(2,1)}), bf16[512,1,128]{2,1,0:T(2,128)(2,1)S(1)}, u32[]{:S(2)}, u32[]{:S(2)}) async-start(bf16[512,1,128]{2,1,0:T(2,128)(2,1)} %copy.24), calls=%async_computation.5 | async-start | bytes 524288 | tf_op jit(solution)/shard_map/all_to_all | solution.py:81
  188.0 14.9 %copy-start.10 = (bf16[128,1024]{1,0:T(8,128)(2,1)S(1)}, bf16[128,1024]{1,0:T(8,128)(2,1)}, u32[]{:S(2)}) copy-start(bf16[128,1024]{1,0:T(8,128)(2,1)} %get-tuple-element.32) | copy-start | bytes 786436
  188.0 14.9 %copy-start.11 = (bf16[128,1024]{1,0:T(8,128)(2,1)S(1)}, bf16[128,1024]{1,0:T(8,128)(2,1)}, u32[]{:S(2)}) copy-start(bf16[128,1024]{1,0:T(8,128)(2,1)} %get-tuple-element.37) | copy-start | bytes 786436
  198.6 6.4 %copy-start.6 = (f32[256,256]{1,0:T(8,128)}, f32[256,256]{1,0:T(8,128)S(1)}, u32[]{:S(2)}) copy-start(f32[256,256]{1,0:T(8,128)S(1)} %convolution_bitcast_fusion.2.coupled_ref) | copy-start | bytes 786436
  205.0 27.3 %all-to-all-start.6 = ((bf16[512,1,128]{2,1,0:T(2,128)(2,1)}), bf16[512,1,128]{2,1,0:T(2,128)(2,1)S(1)}, u32[]{:S(2)}, u32[]{:S(2)}) async-start(bf16[512,1,128]{2,1,0:T(2,128)(2,1)} %all_to_all.83), calls=%async_computation.6 | async-start | bytes 524288 | tf_op jit(solution)/shard_map/all_to_all | solution.py:79
  234.7 25.9 %all-to-all-start.7 = ((bf16[512,1,128]{2,1,0:T(2,128)(2,1)}), bf16[512,1,128]{2,1,0:T(2,128)(2,1)S(1)}, u32[]{:S(2)}, u32[]{:S(2)}) async-start(bf16[512,1,128]{2,1,0:T(2,128)(2,1)} %copy.26), calls=%async_computation.7 | async-start | bytes 524288 | tf_op jit(solution)/shard_map/all_to_all | solution.py:81
  261.7 3.2 copy-start.7
  264.8 8.1 %copy-start.8 = (bf16[1,1,64,1024]{3,2,1,0:T(8,128)(2,1)S(1)}, bf16[1,1,64,1024]{3,2,1,0:T(8,128)(2,1)}, u32[]{:S(2)}) copy-start(bf16[1,1,64,1024]{3,2,1,0:T(8,128)(2,1)} %param.14) | copy-start | bytes 393220

commit v4 on v2

--- a/solution.py
+++ b/solution.py
@@ -77,24 +77,26 @@
     columns = right_side.shape[-1]
     sub_peers = lax.axis_size("sub")
     all_peers = sub_peers * lax.axis_size("region")
+    block_count = inverse.shape[0] // BLK
     residual = right_side[0, 0].astype(jnp.float32)
     accumulated = None
     sent_rows = rows_of(right_side[0, 0], own_blocks[0])
     for colour in range(COLORS):
         picked = own_blocks[colour]
+        if colour + 1 < COLORS:
+            next_inverse_rows = rows_of(inverse, own_blocks[colour + 1])
         received = exchange(sent_rows, partner[colour], all_peers)
         coupled = jnp.dot(tile_set[colour], received, preferred_element_type=jnp.float32)
-        widened = residual
+        block_of_row = lax.broadcasted_iota(jnp.int32, (block_count, 1, 1), 0)
+        added = jnp.zeros((block_count, BLK, columns), jnp.float32)
         for k in range(OVL_BLK):
-            start = picked[k] * BLK
-            block = lax.dynamic_slice_in_dim(widened, start, BLK, axis=0)
-            widened = lax.dynamic_update_slice_in_dim(
-                widened, block + coupled[k * BLK:(k + 1) * BLK], start, axis=0
-            )
+            part = coupled[k * BLK:(k + 1) * BLK][None]
+            added = jnp.where(block_of_row == picked[k], part, added)
+        widened = residual + added.reshape(residual.shape)
         shaped = widened.astype(jnp.bfloat16)
         if colour + 1 < COLORS:
             upcoming = own_blocks[colour + 1]
-            ahead = jnp.dot(rows_of(inverse, upcoming), shaped, preferred_element_type=jnp.float32)
+            ahead = jnp.dot(next_inverse_rows, shaped, preferred_element_type=jnp.float32)
             sent_rows = (rows_of(widened, upcoming) - 0.25 * ahead).astype(jnp.bfloat16)
         accumulated, residual = local_update(inverse, shaped, widened, accumulated)
     settled = residual.astype(jnp.bfloat16)

time: 326 us -> 321 us (0.985)
  other arithmetic: 18 us -> 11.4 us
  matrix products: 6.95 us -> 12.7 us
  waiting for transfers between devices: 118 us -> 113 us
    dynamic_update_slice x8 -> x0, other arithmetic: 9.52 us -> none  [shards(): lax.dynamic_update_slice_in_dim(widened, block + coupled[k * BLK:(k + 1)...]
    eq x0 -> x8, other arithmetic: none -> 5.15 us  [shards(): added = jnp.where(block_of_row == picked[k], part, added)]
    all_to_all x4, waiting for transfers between devices: 62.4 us -> 58.2 us  [exchange(): relayed = lax.all_to_all(pieces, ('region', 'sub'), 0, 0, tiled=True)]
  transfers between devices with their start and end apart: 8 -> 8, of which waited for: 8 -> 8; matrix products, arithmetic and copies ran while one was open for 1% -> 3% of each run, Pallas kernels for 5% -> 5%
where the time goes in v4:
time: 321 us; the launch traced here: 320 us
  waiting for transfers between devices  113 us (35%)
  starting transfers between devices  84.3 us (26%)
  blocking collectives  53.4 us (17%)
  local copies, waits for them, and re-layouts  19.7 us (6%)
  Pallas kernels  19.4 us (6%)
  matrix products  12.7 us (4%)
  other arithmetic  11.4 us (4%)
  between operations  5.87 us (2%)
    all_to_all x4, waiting for transfers between devices, exchange(): relayed = lax.all_to_all(pieces, ('region', 'sub'), 0, 0, tiled=True)  58.2 us
    all_to_all x4, waiting for transfers between devices, exchange(): returned = lax.all_to_all(relayed, ('region', 'sub'), 0, 0, tiled=True)  54.6 us
    all_to_all x1, blocking collectives, shards(): lax.all_to_all(copies, 'sub', 0, 0, tiled=True).reshape(-1, columns)  53.4 us
    all_to_all x4, starting transfers between devices, exchange(): relayed = lax.all_to_all(pieces, ('region', 'sub'), 0, 0, tiled=True)  47.2 us
    all_to_all x4, starting transfers between devices, exchange(): returned = lax.all_to_all(relayed, ('region', 'sub'), 0, 0, tiled=True)  37.1 us
    pallas_call x4, Pallas kernels, local_update(): pl.pallas_call(kernel, out_shape=(out, out), grid=(steps,), in_specs=spec...  19.4 us
  transfers between devices with their start and end apart: 8, of which 8 were waited for; matrix products, arithmetic and copies ran while one was open for 3% of the time, Pallas kernels for 5%

profile of v4, /device:TPU:1, one launch (start us, length us, event | category | flops | bytes accessed | tf_op | source)
XLA Modules:
  0.0 319.6 jit_solution(6234991954990011505)
XLA Ops:
  0.0 1.7 fusion.54
  2.9 0.9 dynamic-slice_bitcast_fusion.7
  4.6 22.1 %all-to-all-start = ((bf16[512,1,128]{2,1,0:T(2,128)(2,1)}), bf16[512,1,128]{2,1,0:T(2,128)(2,1)S(1)}, u32[]{:S(2)}, u32[]{:S(2)}) async-start(bf16[512,1,128]{2,1,0:T(2,128)(2,1)} %all_to_all.80), calls=%async_computation | async-start | bytes 524288 | tf_op jit(solution)/shard_map/all_to_all | solution.py:67
  32.6 0.9 fusion.53
  33.6 2.4 dynamic-slice_bitcast_fusion.1
  36.7 7.4 %all-to-all-done = bf16[512,1,128]{2,1,0:T(2,128)(2,1)S(1)} async-done(((bf16[512,1,128]{2,1,0:T(2,128)(2,1)}), bf16[512,1,128]{2,1,0:T(2,128)(2,1)S(1)}, u32[]{:S(2)}, u32[]{:S(2)}) %all-to-all-start) | async-done | bytes 131104 | tf_op jit(solution)/shard_map/all_to_all | solution.py:67
  44.1 1.3 gather_fusion
  45.6 0.9 copy.34
  46.5 11.9 %all-to-all-start.1 = ((bf16[512,1,128]{2,1,0:T(2,128)(2,1)}), bf16[512,1,128]{2,1,0:T(2,128)(2,1)S(1)}, u32[]{:S(2)}, u32[]{:S(2)}) async-start(bf16[512,1,128]{2,1,0:T(2,128)(2,1)} %copy.34), calls=%async_computation.1 | async-start | bytes 524288 | tf_op jit(solution)/shard_map/all_to_all | solution.py:69
  59.2 16.6 %all-to-all-done.1 = bf16[512,1,128]{2,1,0:T(2,128)(2,1)S(1)} async-done(((bf16[512,1,128]{2,1,0:T(2,128)(2,1)}), bf16[512,1,128]{2,1,0:T(2,128)(2,1)S(1)}, u32[]{:S(2)}, u32[]{:S(2)}) %all-to-all-start.1) | async-done | bytes 131104 | tf_op jit(solution)/shard_map/all_to_all | solution.py:69
  75.8 0.8 reduce
  76.6 1.1 convolution_bitcast_fusion.4
  78.7 0.9 all_to_all.81
  79.6 8.3 %all-to-all-start.2 = ((bf16[512,1,128]{2,1,0:T(2,128)(2,1)}), bf16[512,1,128]{2,1,0:T(2,128)(2,1)S(1)}, u32[]{:S(2)}, u32[]{:S(2)}) async-start(bf16[512,1,128]{2,1,0:T(2,128)(2,1)} %all_to_all.81), calls=%async_computation.2 | async-start | bytes 524288 | tf_op jit(solution)/shard_map/all_to_all | solution.py:67
  88.6 16.9 %all-to-all-done.2 = bf16[512,1,128]{2,1,0:T(2,128)(2,1)S(1)} async-done(((bf16[512,1,128]{2,1,0:T(2,128)(2,1)}), bf16[512,1,128]{2,1,0:T(2,128)(2,1)S(1)}, u32[]{:S(2)}, u32[]{:S(2)}) %all-to-all-start.2) | async-done | bytes 131104 | tf_op jit(solution)/shard_map/all_to_all | solution.py:67
  105.6 1.3 gather_fusion.1
  107.1 0.9 copy.38
  108.0 8.5 %all-to-all-start.3 = ((bf16[512,1,128]{2,1,0:T(2,128)(2,1)}), bf16[512,1,128]{2,1,0:T(2,128)(2,1)S(1)}, u32[]{:S(2)}, u32[]{:S(2)}) async-start(bf16[512,1,128]{2,1,0:T(2,128)(2,1)} %copy.38), calls=%async_computation.3 | async-start | bytes 524288 | tf_op jit(solution)/shard_map/all_to_all | solution.py:69
  116.6 4.7 %shard_map.73 = (f32[1024,256]{1,0:T(8,128)}, f32[1024,256]{1,0:T(8,128)}) custom-call(bf16[1024,1024]{1,0:T(8,128)(2,1)} %bitcast.162, bf16[1024,256]{1,0:T(8,128)(2,1)} %copy-done.6, f32[1024,256]{1,0:T(8,128)} %copy-done.1), custom_call_target="tpu_custom_call" | custom-call | flops 536870912 | bytes 5767168 | tf_op jit(solution)/shard_map/pallas_call | solution.py:47
  121.2 12.9 %all-to-all-done.3 = bf16[512,1,128]{2,1,0:T(2,128)(2,1)S(1)} async-done(((bf16[512,1,128]{2,1,0:T(2,128)(2,1)}), bf16[512,1,128]{2,1,0:T(2,128)(2,1)S(1)}, u32[]{:S(2)}, u32[]{:S(2)}) %all-to-all-start.3) | async-done | bytes 131104 | tf_op jit(solution)/shard_map/all_to_all | solution.py:69
  134.1 0.8 reduce.1
  134.9 1.1 convolution_bitcast_fusion.3
  136.7 1.7 fusion.7
  139.2 8.3 %all-to-all-start.4 = ((bf16[512,1,128]{2,1,0:T(2,128)(2,1)}), bf16[512,1,128]{2,1,0:T(2,128)(2,1)S(1)}, u32[]{:S(2)}, u32[]{:S(2)}) async-start(bf16[512,1,128]{2,1,0:T(2,128)(2,1)} %all_to_all.82), calls=%async_computation.4 | async-start | bytes 524288 | tf_op jit(solution)/shard_map/all_to_all | solution.py:67
  148.1 17.0 %all-to-all-done.4 = bf16[512,1,128]{2,1,0:T(2,128)(2,1)S(1)} async-done(((bf16[512,1,128]{2,1,0:T(2,128)(2,1)}), bf16[512,1,128]{2,1,0:T(2,128)(2,1)S(1)}, u32[]{:S(2)}, u32[]{:S(2)}) %all-to-all-start.4) | async-done | bytes 131104 | tf_op jit(solution)/shard_map/all_to_all | solution.py:67
  165.0 1.3 gather_fusion.2
  166.6 0.9 copy.42
  167.5 8.4 %all-to-all-start.5 = ((bf16[512,1,128]{2,1,0:T(2,128)(2,1)}), bf16[512,1,128]{2,1,0:T(2,128)(2,1)S(1)}, u32[]{:S(2)}, u32[]{:S(2)}) async-start(bf16[512,1,128]{2,1,0:T(2,128)(2,1)} %copy.42), calls=%async_computation.5 | async-start | bytes 524288 | tf_op jit(solution)/shard_map/all_to_all | solution.py:69
  175.9 4.9 %shard_map.74 = (f32[1024,256]{1,0:T(8,128)}, f32[1024,256]{1,0:T(8,128)}) custom-call(bf16[1024,1024]{1,0:T(8,128)(2,1)} %bitcast.163, bf16[1024,256]{1,0:T(8,128)(2,1)} %copy-done.5, f32[1024,256]{1,0:T(8,128)} %copy-done.3, f32[1024,256]{1,0:T(8,128)} %get-tuple-element.15.accumulated_ref), custom_call_target="tpu_custom_call" | custom-call | flops 536870912 | bytes 6815744 | tf_op jit(solution)/shard_map/pallas_call | solution.py:47
  180.8 12.5 %all-to-all-done.5 = bf16[512,1,128]{2,1,0:T(2,128)(2,1)S(1)} async-done(((bf16[512,1,128]{2,1,0:T(2,128)(2,1)}), bf16[512,1,128]{2,1,0:T(2,128)(2,1)S(1)}, u32[]{:S(2)}, u32[]{:S(2)}) %all-to-all-start.5) | async-done | bytes 131104 | tf_op jit(solution)/shard_map/all_to_all | solution.py:69
  193.4 0.8 reduce.2
  194.2 1.1 convolution_bitcast_fusion.2
  196.0 1.7 fusion.6
  197.7 0.8 all_to_all.83
  198.5 8.4 %all-to-all-start.6 = ((bf16[512,1,128]{2,1,0:T(2,128)(2,1)}), bf16[512,1,128]{2,1,0:T(2,128)(2,1)S(1)}, u32[]{:S(2)}, u32[]{:S(2)}) async-start(bf16[512,1,128]{2,1,0:T(2,128)(2,1)} %all_to_all.83), calls=%async_computation.6 | async-start | bytes 524288 | tf_op jit(solution)/shard_map/all_to_all | solution.py:67
  207.6 16.9 %all-to-all-done.6 = bf16[512,1,128]{2,1,0:T(2,128)(2,1)S(1)} async-done(((bf16[512,1,128]{2,1,0:T(2,128)(2,1)}), bf16[512,1,128]{2,1,0:T(2,128)(2,1)S(1)}, u32[]{:S(2)}, u32[]{:S(2)}) %all-to-all-start.6) | async-done | bytes 131104 | tf_op jit(solution)/shard_map/all_to_all | solution.py:67
  224.5 1.3 gather_fusion.3
  226.0 0.9 copy.46
  226.9 8.4 %all-to-all-start.7 = ((bf16[512,1,128]{2,1,0:T(2,128)(2,1)}), bf16[512,1,128]{2,1,0:T(2,128)(2,1)S(1)}, u32[]{:S(2)}, u32[]{:S(2)}) async-start(bf16[512,1,128]{2,1,0:T(2,128)(2,1)} %copy.46), calls=%async_computation.7 | async-start | bytes 524288 | tf_op jit(solution)/shard_map/all_to_all | solution.py:69
  235.3 4.9 %shard_map.75 = (f32[1024,256]{1,0:T(8,128)}, f32[1024,256]{1,0:T(8,128)}) custom-call(bf16[1024,1024]{1,0:T(8,128)(2,1)} %bitcast.164, bf16[1024,256]{1,0:T(8,128)(2,1)} %copy-done.4, f32[1024,256]{1,0:T(8,128)} %copy-done.2, f32[1024,256]{1,0:T(8,128)} %get-tuple-element.17.accumulated_ref), custom_call_target="tpu_custom_call" | custom-call | flops 536870912 | bytes 6815744 | tf_op jit(solution)/shard_map/pallas_call | solution.py:47
  240.3 12.6 %all-to-all-done.7 = bf16[512,1,128]{2,1,0:T(2,128)(2,1)S(1)} async-done(((bf16[512,1,128]{2,1,0:T(2,128)(2,1)}), bf16[512,1,128]{2,1,0:T(2,128)(2,1)S(1)}, u32[]{:S(2)}, u32[]{:S(2)}) %all-to-all-start.7) | async-done | bytes 131104 | tf_op jit(solution)/shard_map/all_to_all | solution.py:69
  252.8 0.8 reduce.3
  253.6 1.1 convolution_bitcast_fusion.1
  255.0 1.5 fusion.43
  256.5 5.0 %shard_map.76 = (f32[1024,256]{1,0:T(8,128)}, f32[1024,256]{1,0:T(8,128)}) custom-call(bf16[1024,1024]{1,0:T(8,128)(2,1)} %bitcast.165, bf16[1024,256]{1,0:T(8,128)(2,1)} %get-tuple-element.22.shaped_ref, f32[1024,256]{1,0:T(8,128)} %get-tuple-element.23.widened_ref, f32[1024,256]{1,0:T(8,128)} %get-tuple-element.19.accumulated_ref), custom_call_target="tpu_custom_call" | custom-call | flops 536870912 | bytes 6815744 | tf_op jit(solution)/shard_map/pallas_call | solution.py:47
  261.5 1.4 fusion.9
  263.2 53.4 %all_to_all.93 = bf16[64,64,256]{2,1,0:T(8,128)(2,1)S(1)} all-to-all(bf16[64,64,256]{2,1,0:T(8,128)(2,1)S(1)} %broadcast_in_dim.200), channel_id=1, replica_groups=mesh['region'=8,'sub'=64] {'sub'}, dimensions={0} | all-to-all | bytes 4194304 | tf_op jit(solution)/shard_map/all_to_all | solution.py:108
  316.6 3.0 fusion.2
  (83 shorter events, 10.4 us)
Async XLA Ops:
  0.0 316.6 %copy-start = (bf16[1,64,4096]{2,1,0:T(8,128)(2,1)S(1)}, bf16[1,64,4096]{2,1,0:T(8,128)(2,1)}, u32[]{:S(2)}) copy-start(bf16[1,64,4096]{2,1,0:T(8,128)(2,1)} %param.15) | copy-start | bytes 1572868
  4.6 39.5 %all-to-all-start = ((bf16[512,1,128]{2,1,0:T(2,128)(2,1)}), bf16[512,1,128]{2,1,0:T(2,128)(2,1)S(1)}, u32[]{:S(2)}, u32[]{:S(2)}) async-start(bf16[512,1,128]{2,1,0:T(2,128)(2,1)} %all_to_all.80), calls=%async_computation | async-start | bytes 524288 | tf_op jit(solution)/shard_map/all_to_all | solution.py:67
  44.1 33.9 %copy-start.10 = (bf16[1,1,1024,256]{3,2,1,0:T(8,128)(2,1)S(1)}, bf16[1,1,1024,256]{3,2,1,0:T(8,128)(2,1)}, u32[]{:S(2)}) copy-start(bf16[1,1,1024,256]{3,2,1,0:T(8,128)(2,1)} %param.9) | copy-start | bytes 1572868
  46.5 29.3 %all-to-all-start.1 = ((bf16[512,1,128]{2,1,0:T(2,128)(2,1)}), bf16[512,1,128]{2,1,0:T(2,128)(2,1)S(1)}, u32[]{:S(2)}, u32[]{:S(2)}) async-start(bf16[512,1,128]{2,1,0:T(2,128)(2,1)} %copy.34), calls=%async_computation.1 | async-start | bytes 524288 | tf_op jit(solution)/shard_map/all_to_all | solution.py:69
  78.4 28.6 %copy-start.1 = (f32[1024,256]{1,0:T(8,128)}, f32[1024,256]{1,0:T(8,128)S(1)}, u32[]{:S(2)}) copy-start(f32[1024,256]{1,0:T(8,128)S(1)} %get-tuple-element.40.widened_ref) | copy-start | bytes 3145732
  78.4 28.6 %copy-start.6 = (bf16[1024,256]{1,0:T(8,128)(2,1)}, bf16[1024,256]{1,0:T(8,128)(2,1)S(1)}, u32[]{:S(2)}) copy-start(bf16[1024,256]{1,0:T(8,128)(2,1)S(1)} %get-tuple-element.41.shaped_ref) | copy-start | bytes 1572868
  79.6 26.0 %all-to-all-start.2 = ((bf16[512,1,128]{2,1,0:T(2,128)(2,1)}), bf16[512,1,128]{2,1,0:T(2,128)(2,1)S(1)}, u32[]{:S(2)}, u32[]{:S(2)}) async-start(bf16[512,1,128]{2,1,0:T(2,128)(2,1)} %all_to_all.81), calls=%async_computation.2 | async-start | bytes 524288 | tf_op jit(solution)/shard_map/all_to_all | solution.py:67
  108.0 26.1 %all-to-all-start.3 = ((bf16[512,1,128]{2,1,0:T(2,128)(2,1)}), bf16[512,1,128]{2,1,0:T(2,128)(2,1)S(1)}, u32[]{:S(2)}, u32[]{:S(2)}) async-start(bf16[512,1,128]{2,1,0:T(2,128)(2,1)} %copy.38), calls=%async_computation.3 | async-start | bytes 524288 | tf_op jit(solution)/shard_map/all_to_all | solution.py:69
  121.2 15.1 %copy-start.9 = (f32[1024,256]{1,0:T(8,128)S(1)}, f32[1024,256]{1,0:T(8,128)}, u32[]{:S(2)}) copy-start(f32[1024,256]{1,0:T(8,128)} %get-tuple-element.14) | copy-start | bytes 3145732
  136.6 29.8 %copy-start.3 = (f32[1024,256]{1,0:T(8,128)}, f32[1024,256]{1,0:T(8,128)S(1)}, u32[]{:S(2)}) copy-start(f32[1024,256]{1,0:T(8,128)S(1)} %get-tuple-element.27.widened_ref) | copy-start | bytes 3145732
  136.6 29.8 %copy-start.5 = (bf16[1024,256]{1,0:T(8,128)(2,1)}, bf16[1024,256]{1,0:T(8,128)(2,1)S(1)}, u32[]{:S(2)}) copy-start(bf16[1024,256]{1,0:T(8,128)(2,1)S(1)} %get-tuple-element.26.shaped_ref) | copy-start | bytes 1572868
  139.2 25.9 %all-to-all-start.4 = ((bf16[512,1,128]{2,1,0:T(2,128)(2,1)}), bf16[512,1,128]{2,1,0:T(2,128)(2,1)S(1)}, u32[]{:S(2)}, u32[]{:S(2)}) async-start(bf16[512,1,128]{2,1,0:T(2,128)(2,1)} %all_to_all.82), calls=%async_computation.4 | async-start | bytes 524288 | tf_op jit(solution)/shard_map/all_to_all | solution.py:67
  167.5 25.9 %all-to-all-start.5 = ((bf16[512,1,128]{2,1,0:T(2,128)(2,1)}), bf16[512,1,128]{2,1,0:T(2,128)(2,1)S(1)}, u32[]{:S(2)}, u32[]{:S(2)}) async-start(bf16[512,1,128]{2,1,0:T(2,128)(2,1)} %copy.42), calls=%async_computation.5 | async-start | bytes 524288 | tf_op jit(solution)/shard_map/all_to_all | solution.py:69
  180.8 14.7 %copy-start.8 = (f32[1024,256]{1,0:T(8,128)S(1)}, f32[1024,256]{1,0:T(8,128)}, u32[]{:S(2)}) copy-start(f32[1024,256]{1,0:T(8,128)} %get-tuple-element.16) | copy-start | bytes 3145732
  195.9 29.9 %copy-start.2 = (f32[1024,256]{1,0:T(8,128)}, f32[1024,256]{1,0:T(8,128)S(1)}, u32[]{:S(2)}) copy-start(f32[1024,256]{1,0:T(8,128)S(1)} %get-tuple-element.25.widened_ref) | copy-start | bytes 3145732
  195.9 29.9 %copy-start.4 = (bf16[1024,256]{1,0:T(8,128)(2,1)}, bf16[1024,256]{1,0:T(8,128)(2,1)S(1)}, u32[]{:S(2)}) copy-start(bf16[1024,256]{1,0:T(8,128)(2,1)S(1)} %get-tuple-element.24.shaped_ref) | copy-start | bytes 1572868
  198.5 26.0 %all-to-all-start.6 = ((bf16[512,1,128]{2,1,0:T(2,128)(2,1)}), bf16[512,1,128]{2,1,0:T(2,128)(2,1)S(1)}, u32[]{:S(2)}, u32[]{:S(2)}) async-start(bf16[512,1,128]{2,1,0:T(2,128)(2,1)} %all_to_all.83), calls=%async_computation.6 | async-start | bytes 524288 | tf_op jit(solution)/shard_map/all_to_all | solution.py:67
  226.9 25.9 %all-to-all-start.7 = ((bf16[512,1,128]{2,1,0:T(2,128)(2,1)}), bf16[512,1,128]{2,1,0:T(2,128)(2,1)S(1)}, u32[]{:S(2)}, u32[]{:S(2)}) async-start(bf16[512,1,128]{2,1,0:T(2,128)(2,1)} %copy.46), calls=%async_computation.7 | async-start | bytes 524288 | tf_op jit(solution)/shard_map/all_to_all | solution.py:69
  240.3 14.8 %copy-start.7 = (f32[1024,256]{1,0:T(8,128)S(1)}, f32[1024,256]{1,0:T(8,128)}, u32[]{:S(2)}) copy-start(f32[1024,256]{1,0:T(8,128)} %get-tuple-element.18) | copy-start | bytes 3145732
  256.5 5.0 %copy-start.11 = (bf16[1,1,64,1024]{3,2,1,0:T(8,128)(2,1)S(1)}, bf16[1,1,64,1024]{3,2,1,0:T(8,128)(2,1)}, u32[]{:S(2)}) copy-start(bf16[1,1,64,1024]{3,2,1,0:T(8,128)(2,1)} %param.14) | copy-start | bytes 393220

commit v5 on v4

--- a/solution.py
+++ b/solution.py
@@ -70,6 +70,19 @@
     return returned.reshape(span_rows, columns)
 
 
+def gather_rows(block, peers):
+    bits = peers.bit_length() - 1
+    me = lax.axis_index("sub")
+    held = block[None]
+    for bit in reversed(range(bits)):
+        other = lax.ppermute(held, "sub", [(i, i ^ (1 << bit)) for i in range(peers)])
+        low = (me >> bit) & 1 == 0
+        held = jnp.stack([jnp.where(low, held, other), jnp.where(low, other, held)], axis=0)
+    held = held.reshape((2,) * bits + block.shape)
+    held = jnp.transpose(held, tuple(reversed(range(bits))) + (bits, bits + 1))
+    return held.reshape(peers * block.shape[0], block.shape[1])
+
+
 def shards(right_side, local_inverse, coupling, margin_blocks, partner, restriction, coarse_rows):
     inverse = local_inverse[0, 0]
     tile_set = coupling[0, 0]
@@ -104,8 +117,7 @@
     projected = jnp.dot(own_restriction, settled, preferred_element_type=jnp.float32).astype(
         jnp.bfloat16
     )
-    copies = jnp.broadcast_to(projected[None], (sub_peers,) + projected.shape)
-    gathered = lax.all_to_all(copies, "sub", 0, 0, tiled=True).reshape(-1, columns)
+    gathered = gather_rows(projected, sub_peers)
     coarse = jnp.dot(coarse_rows[0], gathered, preferred_element_type=jnp.float32).astype(
         jnp.bfloat16
     )

time: 321 us -> 319 us (level)
  blocking collectives: 53.4 us -> 0 us
  waiting for transfers between devices: 113 us -> 146 us
  starting transfers between devices: 84.3 us -> 101 us
    all_to_all x1 -> x0, blocking collectives: 53.4 us -> none  [shards(): lax.all_to_all(copies, 'sub', 0, 0, tiled=True).reshape(-1, columns)]
    ppermute x0 -> x6, waiting for transfers between devices: none -> 32.9 us  [gather_rows(): other = lax.ppermute(held, 'sub', [(i, i ^ 1 << bit) for i in range(peers)])]
    ppermute x0 -> x6, starting transfers between devices: none -> 17.2 us  [gather_rows(): other = lax.ppermute(held, 'sub', [(i, i ^ 1 << bit) for i in range(peers)])]
  transfers between devices with their start and end apart: 8 -> 14, of which waited for: 8 -> 14; matrix products, arithmetic and copies ran while one was open for 3% -> 3% of each run, Pallas kernels for 5% -> 5%
where the time goes in v5:
time: 319 us; the launch traced here: 318 us
  waiting for transfers between devices  146 us (46%)
  starting transfers between devices  101 us (32%)
  Pallas kernels  19.7 us (6%)
  local copies, waits for them, and re-layouts  19.6 us (6%)
  other arithmetic  13 us (4%)
  matrix products  12.7 us (4%)
  between operations  5.78 us (2%)
    all_to_all x4, waiting for transfers between devices, exchange(): relayed = lax.all_to_all(pieces, ('region', 'sub'), 0, 0, tiled=True)  58.7 us
    all_to_all x4, waiting for transfers between devices, exchange(): returned = lax.all_to_all(relayed, ('region', 'sub'), 0, 0, tiled=True)  54.3 us
    all_to_all x4, starting transfers between devices, exchange(): relayed = lax.all_to_all(pieces, ('region', 'sub'), 0, 0, tiled=True)  47.2 us
    all_to_all x4, starting transfers between devices, exchange(): returned = lax.all_to_all(relayed, ('region', 'sub'), 0, 0, tiled=True)  36.7 us
    ppermute x6, waiting for transfers between devices, gather_rows(): other = lax.ppermute(held, 'sub', [(i, i ^ 1 << bit) for i in range(peers)])  32.9 us
    pallas_call x4, Pallas kernels, local_update(): pl.pallas_call(kernel, out_shape=(out, out), grid=(steps,), in_specs=spec...  19.7 us
    ppermute x6, starting transfers between devices, gather_rows(): other = lax.ppermute(held, 'sub', [(i, i ^ 1 << bit) for i in range(peers)])  17.2 us
  transfers between devices with their start and end apart: 14, of which 14 were waited for; matrix products, arithmetic and copies ran while one was open for 3% of the time, Pallas kernels for 5%

profile of v5, /device:TPU:1, one launch (start us, length us, event | category | flops | bytes accessed | tf_op | source)
XLA Modules:
  0.0 317.7 jit_solution(4394319874370507698)
XLA Ops:
  0.0 1.6 fusion.64
  4.6 22.1 %all-to-all-start = ((bf16[512,1,128]{2,1,0:T(2,128)(2,1)}), bf16[512,1,128]{2,1,0:T(2,128)(2,1)S(1)}, u32[]{:S(2)}, u32[]{:S(2)}) async-start(bf16[512,1,128]{2,1,0:T(2,128)(2,1)} %all_to_all.76), calls=%async_computation | async-start | bytes 524288 | tf_op jit(solution)/shard_map/all_to_all | solution.py:67
  33.1 2.4 dynamic-slice_bitcast_fusion.1
  36.2 7.9 %all-to-all-done = bf16[512,1,128]{2,1,0:T(2,128)(2,1)S(1)} async-done(((bf16[512,1,128]{2,1,0:T(2,128)(2,1)}), bf16[512,1,128]{2,1,0:T(2,128)(2,1)S(1)}, u32[]{:S(2)}, u32[]{:S(2)}) %all-to-all-start) | async-done | bytes 131104 | tf_op jit(solution)/shard_map/all_to_all | solution.py:67
  44.2 1.3 gather_fusion
  46.6 11.4 %all-to-all-start.1 = ((bf16[512,1,128]{2,1,0:T(2,128)(2,1)}), bf16[512,1,128]{2,1,0:T(2,128)(2,1)S(1)}, u32[]{:S(2)}, u32[]{:S(2)}) async-start(bf16[512,1,128]{2,1,0:T(2,128)(2,1)} %copy.105), calls=%async_computation.1 | async-start | bytes 524288 | tf_op jit(solution)/shard_map/all_to_all | solution.py:69
  58.8 16.6 %all-to-all-done.1 = bf16[512,1,128]{2,1,0:T(2,128)(2,1)S(1)} async-done(((bf16[512,1,128]{2,1,0:T(2,128)(2,1)}), bf16[512,1,128]{2,1,0:T(2,128)(2,1)S(1)}, u32[]{:S(2)}, u32[]{:S(2)}) %all-to-all-start.1) | async-done | bytes 131104 | tf_op jit(solution)/shard_map/all_to_all | solution.py:69
  76.2 1.1 convolution_bitcast_fusion.4
  79.1 8.4 %all-to-all-start.2 = ((bf16[512,1,128]{2,1,0:T(2,128)(2,1)}), bf16[512,1,128]{2,1,0:T(2,128)(2,1)S(1)}, u32[]{:S(2)}, u32[]{:S(2)}) async-start(bf16[512,1,128]{2,1,0:T(2,128)(2,1)} %all_to_all.77), calls=%async_computation.2 | async-start | bytes 524288 | tf_op jit(solution)/shard_map/all_to_all | solution.py:67
  88.1 17.0 %all-to-all-done.2 = bf16[512,1,128]{2,1,0:T(2,128)(2,1)S(1)} async-done(((bf16[512,1,128]{2,1,0:T(2,128)(2,1)}), bf16[512,1,128]{2,1,0:T(2,128)(2,1)S(1)}, u32[]{:S(2)}, u32[]{:S(2)}) %all-to-all-start.2) | async-done | bytes 131104 | tf_op jit(solution)/shard_map/all_to_all | solution.py:67
  105.1 1.3 gather_fusion.1
  107.5 8.5 %all-to-all-start.3 = ((bf16[512,1,128]{2,1,0:T(2,128)(2,1)}), bf16[512,1,128]{2,1,0:T(2,128)(2,1)S(1)}, u32[]{:S(2)}, u32[]{:S(2)}) async-start(bf16[512,1,128]{2,1,0:T(2,128)(2,1)} %copy.109), calls=%async_computation.3 | async-start | bytes 524288 | tf_op jit(solution)/shard_map/all_to_all | solution.py:69
  116.1 4.7 %shard_map.73 = (f32[1024,256]{1,0:T(8,128)}, f32[1024,256]{1,0:T(8,128)}) custom-call(bf16[1024,1024]{1,0:T(8,128)(2,1)} %bitcast.247, bf16[1024,256]{1,0:T(8,128)(2,1)} %copy-done.6, f32[1024,256]{1,0:T(8,128)} %copy-done.1), custom_call_target="tpu_custom_call" | custom-call | flops 536870912 | bytes 5767168 | tf_op jit(solution)/shard_map/pallas_call | solution.py:47
  120.8 12.7 %all-to-all-done.3 = bf16[512,1,128]{2,1,0:T(2,128)(2,1)S(1)} async-done(((bf16[512,1,128]{2,1,0:T(2,128)(2,1)}), bf16[512,1,128]{2,1,0:T(2,128)(2,1)S(1)}, u32[]{:S(2)}, u32[]{:S(2)}) %all-to-all-start.3) | async-done | bytes 131104 | tf_op jit(solution)/shard_map/all_to_all | solution.py:69
  134.3 1.1 convolution_bitcast_fusion.3
  136.1 1.7 fusion.7
  138.6 8.4 %all-to-all-start.4 = ((bf16[512,1,128]{2,1,0:T(2,128)(2,1)}), bf16[512,1,128]{2,1,0:T(2,128)(2,1)S(1)}, u32[]{:S(2)}, u32[]{:S(2)}) async-start(bf16[512,1,128]{2,1,0:T(2,128)(2,1)} %all_to_all.78), calls=%async_computation.4 | async-start | bytes 524288 | tf_op jit(solution)/shard_map/all_to_all | solution.py:67
  147.6 16.9 %all-to-all-done.4 = bf16[512,1,128]{2,1,0:T(2,128)(2,1)S(1)} async-done(((bf16[512,1,128]{2,1,0:T(2,128)(2,1)}), bf16[512,1,128]{2,1,0:T(2,128)(2,1)S(1)}, u32[]{:S(2)}, u32[]{:S(2)}) %all-to-all-start.4) | async-done | bytes 131104 | tf_op jit(solution)/shard_map/all_to_all | solution.py:67
  164.5 1.3 gather_fusion.2
  166.9 8.3 %all-to-all-start.5 = ((bf16[512,1,128]{2,1,0:T(2,128)(2,1)}), bf16[512,1,128]{2,1,0:T(2,128)(2,1)S(1)}, u32[]{:S(2)}, u32[]{:S(2)}) async-start(bf16[512,1,128]{2,1,0:T(2,128)(2,1)} %copy.113), calls=%async_computation.5 | async-start | bytes 524288 | tf_op jit(solution)/shard_map/all_to_all | solution.py:69
  175.4 5.0 %shard_map.74 = (f32[1024,256]{1,0:T(8,128)}, f32[1024,256]{1,0:T(8,128)}) custom-call(bf16[1024,1024]{1,0:T(8,128)(2,1)} %bitcast.248, bf16[1024,256]{1,0:T(8,128)(2,1)} %copy-done.5, f32[1024,256]{1,0:T(8,128)} %copy-done.3, f32[1024,256]{1,0:T(8,128)} %get-tuple-element.15.accumulated_ref), custom_call_target="tpu_custom_call" | custom-call | flops 536870912 | bytes 6815744 | tf_op jit(solution)/shard_map/pallas_call | solution.py:47
  180.4 12.5 %all-to-all-done.5 = bf16[512,1,128]{2,1,0:T(2,128)(2,1)S(1)} async-done(((bf16[512,1,128]{2,1,0:T(2,128)(2,1)}), bf16[512,1,128]{2,1,0:T(2,128)(2,1)S(1)}, u32[]{:S(2)}, u32[]{:S(2)}) %all-to-all-start.5) | async-done | bytes 131104 | tf_op jit(solution)/shard_map/all_to_all | solution.py:69
  193.7 1.1 convolution_bitcast_fusion.2
  195.4 1.7 fusion.6
  197.9 8.3 %all-to-all-start.6 = ((bf16[512,1,128]{2,1,0:T(2,128)(2,1)}), bf16[512,1,128]{2,1,0:T(2,128)(2,1)S(1)}, u32[]{:S(2)}, u32[]{:S(2)}) async-start(bf16[512,1,128]{2,1,0:T(2,128)(2,1)} %all_to_all.79), calls=%async_computation.6 | async-start | bytes 524288 | tf_op jit(solution)/shard_map/all_to_all | solution.py:67
  206.9 16.9 %all-to-all-done.6 = bf16[512,1,128]{2,1,0:T(2,128)(2,1)S(1)} async-done(((bf16[512,1,128]{2,1,0:T(2,128)(2,1)}), bf16[512,1,128]{2,1,0:T(2,128)(2,1)S(1)}, u32[]{:S(2)}, u32[]{:S(2)}) %all-to-all-start.6) | async-done | bytes 131104 | tf_op jit(solution)/shard_map/all_to_all | solution.py:67
  223.8 1.3 gather_fusion.3
  226.3 8.4 %all-to-all-start.7 = ((bf16[512,1,128]{2,1,0:T(2,128)(2,1)}), bf16[512,1,128]{2,1,0:T(2,128)(2,1)S(1)}, u32[]{:S(2)}, u32[]{:S(2)}) async-start(bf16[512,1,128]{2,1,0:T(2,128)(2,1)} %copy.117), calls=%async_computation.7 | async-start | bytes 524288 | tf_op jit(solution)/shard_map/all_to_all | solution.py:69
  234.7 4.9 %shard_map.75 = (f32[1024,256]{1,0:T(8,128)}, f32[1024,256]{1,0:T(8,128)}) custom-call(bf16[1024,1024]{1,0:T(8,128)(2,1)} %bitcast.249, bf16[1024,256]{1,0:T(8,128)(2,1)} %copy-done.4, f32[1024,256]{1,0:T(8,128)} %copy-done.2, f32[1024,256]{1,0:T(8,128)} %get-tuple-element.17.accumulated_ref), custom_call_target="tpu_custom_call" | custom-call | flops 536870912 | bytes 6815744 | tf_op jit(solution)/shard_map/pallas_call | solution.py:47
  239.7 12.5 %all-to-all-done.7 = bf16[512,1,128]{2,1,0:T(2,128)(2,1)S(1)} async-done(((bf16[512,1,128]{2,1,0:T(2,128)(2,1)}), bf16[512,1,128]{2,1,0:T(2,128)(2,1)S(1)}, u32[]{:S(2)}, u32[]{:S(2)}) %all-to-all-start.7) | async-done | bytes 131104 | tf_op jit(solution)/shard_map/all_to_all | solution.py:69
  253.0 1.1 convolution_bitcast_fusion.1
  254.4 1.5 fusion.53
  255.9 5.0 %shard_map.76 = (f32[1024,256]{1,0:T(8,128)}, f32[1024,256]{1,0:T(8,128)}) custom-call(bf16[1024,1024]{1,0:T(8,128)(2,1)} %bitcast.250, bf16[1024,256]{1,0:T(8,128)(2,1)} %get-tuple-element.22.shaped_ref, f32[1024,256]{1,0:T(8,128)} %get-tuple-element.23.widened_ref, f32[1024,256]{1,0:T(8,128)} %get-tuple-element.19.accumulated_ref), custom_call_target="tpu_custom_call" | custom-call | flops 536870912 | bytes 6815744 | tf_op jit(solution)/shard_map/pallas_call | solution.py:47
  260.9 1.4 fusion.9
  262.3 2.2 collective-permute-start
  264.6 6.4 %collective-permute-done = bf16[1,64,256]{2,1,0:T(8,128)(2,1)S(1)} collective-permute-done((bf16[1,64,256]{2,1,0:T(8,128)(2,1)S(1)}, bf16[1,64,256]{2,1,0:T(8,128)(2,1)S(1)}, u32[]{:S(2)}, u32[]{:S(2)}) %collective-permute-start) | collective-permute-done | bytes 32800 | tf_op jit(solution)/shard_map/ppermute | solution.py:78
  271.0 2.0 collective-permute-start.1
  273.0 4.6 %collective-permute-done.1 = bf16[2,1,64,256]{3,2,0,1:T(8,128)(2,1)S(1)} collective-permute-done((bf16[2,1,64,256]{3,2,0,1:T(8,128)(2,1)S(1)}, bf16[2,1,64,256]{3,2,0,1:T(8,128)(2,1)S(1)}, u32[]{:S(2)}, u32[]{:S(2)}) %collective-permute-start.1) | collective-permute-done | bytes 65568 | tf_op jit(solution)/shard_map/ppermute | solution.py:78
  277.6 1.9 collective-permute-start.2
  279.6 3.8 %collective-permute-done.2 = bf16[2,2,1,64,256]{4,3,1,0,2:T(8,128)(2,1)S(1)} collective-permute-done((bf16[2,2,1,64,256]{4,3,1,0,2:T(8,128)(2,1)S(1)}, bf16[2,2,1,64,256]{4,3,1,0,2:T(8,128)(2,1)S(1)}, u32[]{:S(2)}, u32[]{:S(2)}) %collective-permute-start.2) | collective-permute-done | bytes 131104 | tf_op jit(solution)/shard_map/ppermute | solution.py:78
  283.4 1.9 collective-permute-start.3
  285.4 6.7 %collective-permute-done.3 = bf16[2,2,2,1,64,256]{5,4,2,1,0,3:T(8,128)(2,1)S(1)} collective-permute-done((bf16[2,2,2,1,64,256]{5,4,2,1,0,3:T(8,128)(2,1)S(1)}, bf16[2,2,2,1,64,256]{5,4,2,1,0,3:T(8,128)(2,1)S(1)}, u32[]{:S(2)}, u32[]{:S(2)}) %collective-permute-start.3) | collective-permute-done | bytes 262176 | tf_op jit(solution)/shard_map/ppermute | solution.py:78
  292.2 2.3 collective-permute-start.4
  294.5 9.0 %collective-permute-done.4 = bf16[2,2,2,2,1,64,256]{6,5,3,2,1,0,4:T(8,128)(2,1)S(1)} collective-permute-done((bf16[2,2,2,2,1,64,256]{6,5,3,2,1,0,4:T(8,128)(2,1)S(1)}, bf16[2,2,2,2,1,64,256]{6,5,3,2,1,0,4:T(8,128)(2,1)S(1)}, u32[]{:S(2)}, u32[]{:S(2)}) %collective-permute-start.4) | collective-permute-done | bytes 524320 | tf_op jit(solution)/shard_map/ppermute | solution.py:78
  303.6 1.1 fusion.18
  304.7 6.9 %collective-permute-start.5 = (bf16[2,2,2,2,2,1,64,256]{7,6,4,3,2,1,0,5:T(8,128)(2,1)}, bf16[2,2,2,2,2,1,64,256]{7,6,4,3,2,1,0,5:T(8,128)(2,1)S(1)}, u32[]{:S(2)}, u32[]{:S(2)}) collective-permute-start(bf16[2,2,2,2,2,1,64,256]{7,6,4,3,2,1,0,5:T(8,128)(2,1)} %fusion.18), channel_id=1, source_target_pairs={{0,1},{1,0},{2,3},{3,2},{4,5},{5,4},{6,7},{7,6},{8,9},{9,8},{10,11... | collective-permute-start | bytes 3145736 | tf_op jit(solution)/shard_map/ppermute | solution.py:78
  311.6 2.5 collective-permute-done.5
  314.7 3.0 fusion.2
  (111 shorter events, 21.0 us)
Async XLA Ops:
  0.0 314.7 %copy-start = (bf16[1,64,4096]{2,1,0:T(8,128)(2,1)S(1)}, bf16[1,64,4096]{2,1,0:T(8,128)(2,1)}, u32[]{:S(2)}) copy-start(bf16[1,64,4096]{2,1,0:T(8,128)(2,1)} %param.15) | copy-start | bytes 1572868
  4.6 39.5 %all-to-all-start = ((bf16[512,1,128]{2,1,0:T(2,128)(2,1)}), bf16[512,1,128]{2,1,0:T(2,128)(2,1)S(1)}, u32[]{:S(2)}, u32[]{:S(2)}) async-start(bf16[512,1,128]{2,1,0:T(2,128)(2,1)} %all_to_all.76), calls=%async_computation | async-start | bytes 524288 | tf_op jit(solution)/shard_map/all_to_all | solution.py:67
  44.1 33.4 %copy-start.10 = (bf16[1,1,1024,256]{3,2,1,0:T(8,128)(2,1)S(1)}, bf16[1,1,1024,256]{3,2,1,0:T(8,128)(2,1)}, u32[]{:S(2)}) copy-start(bf16[1,1,1024,256]{3,2,1,0:T(8,128)(2,1)} %param.9) | copy-start | bytes 1572868
  46.6 28.8 %all-to-all-start.1 = ((bf16[512,1,128]{2,1,0:T(2,128)(2,1)}), bf16[512,1,128]{2,1,0:T(2,128)(2,1)S(1)}, u32[]{:S(2)}, u32[]{:S(2)}) async-start(bf16[512,1,128]{2,1,0:T(2,128)(2,1)} %copy.105), calls=%async_computation.1 | async-start | bytes 524288 | tf_op jit(solution)/shard_map/all_to_all | solution.py:69
  77.9 28.5 %copy-start.1 = (f32[1024,256]{1,0:T(8,128)}, f32[1024,256]{1,0:T(8,128)S(1)}, u32[]{:S(2)}) copy-start(f32[1024,256]{1,0:T(8,128)S(1)} %get-tuple-element.40.widened_ref) | copy-start | bytes 3145732
  77.9 28.5 %copy-start.6 = (bf16[1024,256]{1,0:T(8,128)(2,1)}, bf16[1024,256]{1,0:T(8,128)(2,1)S(1)}, u32[]{:S(2)}) copy-start(bf16[1024,256]{1,0:T(8,128)(2,1)S(1)} %get-tuple-element.41.shaped_ref) | copy-start | bytes 1572868
  79.1 25.9 %all-to-all-start.2 = ((bf16[512,1,128]{2,1,0:T(2,128)(2,1)}), bf16[512,1,128]{2,1,0:T(2,128)(2,1)S(1)}, u32[]{:S(2)}, u32[]{:S(2)}) async-start(bf16[512,1,128]{2,1,0:T(2,128)(2,1)} %all_to_all.77), calls=%async_computation.2 | async-start | bytes 524288 | tf_op jit(solution)/shard_map/all_to_all | solution.py:67
  107.5 26.0 %all-to-all-start.3 = ((bf16[512,1,128]{2,1,0:T(2,128)(2,1)}), bf16[512,1,128]{2,1,0:T(2,128)(2,1)S(1)}, u32[]{:S(2)}, u32[]{:S(2)}) async-start(bf16[512,1,128]{2,1,0:T(2,128)(2,1)} %copy.109), calls=%async_computation.3 | async-start | bytes 524288 | tf_op jit(solution)/shard_map/all_to_all | solution.py:69
  120.8 14.9 %copy-start.9 = (f32[1024,256]{1,0:T(8,128)S(1)}, f32[1024,256]{1,0:T(8,128)}, u32[]{:S(2)}) copy-start(f32[1024,256]{1,0:T(8,128)} %get-tuple-element.14) | copy-start | bytes 3145732
  136.1 29.8 %copy-start.3 = (f32[1024,256]{1,0:T(8,128)}, f32[1024,256]{1,0:T(8,128)S(1)}, u32[]{:S(2)}) copy-start(f32[1024,256]{1,0:T(8,128)S(1)} %get-tuple-element.27.widened_ref) | copy-start | bytes 3145732
  136.1 29.8 %copy-start.5 = (bf16[1024,256]{1,0:T(8,128)(2,1)}, bf16[1024,256]{1,0:T(8,128)(2,1)S(1)}, u32[]{:S(2)}) copy-start(bf16[1024,256]{1,0:T(8,128)(2,1)S(1)} %get-tuple-element.26.shaped_ref) | copy-start | bytes 1572868
  138.6 25.8 %all-to-all-start.4 = ((bf16[512,1,128]{2,1,0:T(2,128)(2,1)}), bf16[512,1,128]{2,1,0:T(2,128)(2,1)S(1)}, u32[]{:S(2)}, u32[]{:S(2)}) async-start(bf16[512,1,128]{2,1,0:T(2,128)(2,1)} %all_to_all.78), calls=%async_computation.4 | async-start | bytes 524288 | tf_op jit(solution)/shard_map/all_to_all | solution.py:67
  166.9 25.9 %all-to-all-start.5 = ((bf16[512,1,128]{2,1,0:T(2,128)(2,1)}), bf16[512,1,128]{2,1,0:T(2,128)(2,1)S(1)}, u32[]{:S(2)}, u32[]{:S(2)}) async-start(bf16[512,1,128]{2,1,0:T(2,128)(2,1)} %copy.113), calls=%async_computation.5 | async-start | bytes 524288 | tf_op jit(solution)/shard_map/all_to_all | solution.py:69
  180.4 14.7 %copy-start.8 = (f32[1024,256]{1,0:T(8,128)S(1)}, f32[1024,256]{1,0:T(8,128)}, u32[]{:S(2)}) copy-start(f32[1024,256]{1,0:T(8,128)} %get-tuple-element.16) | copy-start | bytes 3145732
  195.4 29.8 %copy-start.2 = (f32[1024,256]{1,0:T(8,128)}, f32[1024,256]{1,0:T(8,128)S(1)}, u32[]{:S(2)}) copy-start(f32[1024,256]{1,0:T(8,128)S(1)} %get-tuple-element.25.widened_ref) | copy-start | bytes 3145732
  195.4 29.8 %copy-start.4 = (bf16[1024,256]{1,0:T(8,128)(2,1)}, bf16[1024,256]{1,0:T(8,128)(2,1)S(1)}, u32[]{:S(2)}) copy-start(bf16[1024,256]{1,0:T(8,128)(2,1)S(1)} %get-tuple-element.24.shaped_ref) | copy-start | bytes 1572868
  197.9 25.9 %all-to-all-start.6 = ((bf16[512,1,128]{2,1,0:T(2,128)(2,1)}), bf16[512,1,128]{2,1,0:T(2,128)(2,1)S(1)}, u32[]{:S(2)}, u32[]{:S(2)}) async-start(bf16[512,1,128]{2,1,0:T(2,128)(2,1)} %all_to_all.79), calls=%async_computation.6 | async-start | bytes 524288 | tf_op jit(solution)/shard_map/all_to_all | solution.py:67
  226.3 25.9 %all-to-all-start.7 = ((bf16[512,1,128]{2,1,0:T(2,128)(2,1)}), bf16[512,1,128]{2,1,0:T(2,128)(2,1)S(1)}, u32[]{:S(2)}, u32[]{:S(2)}) async-start(bf16[512,1,128]{2,1,0:T(2,128)(2,1)} %copy.117), calls=%async_computation.7 | async-start | bytes 524288 | tf_op jit(solution)/shard_map/all_to_all | solution.py:69
  239.7 14.7 %copy-start.7 = (f32[1024,256]{1,0:T(8,128)S(1)}, f32[1024,256]{1,0:T(8,128)}, u32[]{:S(2)}) copy-start(f32[1024,256]{1,0:T(8,128)} %get-tuple-element.18) | copy-start | bytes 3145732
  255.9 5.0 %copy-start.11 = (bf16[1,1,64,1024]{3,2,1,0:T(8,128)(2,1)S(1)}, bf16[1,1,64,1024]{3,2,1,0:T(8,128)(2,1)}, u32[]{:S(2)}) copy-start(bf16[1,1,64,1024]{3,2,1,0:T(8,128)(2,1)} %param.14) | copy-start | bytes 393220
  262.3 8.6 %collective-permute-start = (bf16[1,64,256]{2,1,0:T(8,128)(2,1)S(1)}, bf16[1,64,256]{2,1,0:T(8,128)(2,1)S(1)}, u32[]{:S(2)}, u32[]{:S(2)}) collective-permute-start(bf16[1,64,256]{2,1,0:T(8,128)(2,1)S(1)} %fusion.9), channel_id=1, source_target_pairs={{0,32},{1,33},{2,34},{3,35},{4,36},{5,37},{6,38},{7,39},{8,40},{9,... | collective-permute-start | bytes 98312 | tf_op jit(solution)/shard_map/ppermute | solution.py:78
  271.0 6.6 %collective-permute-start.1 = (bf16[2,1,64,256]{3,2,0,1:T(8,128)(2,1)S(1)}, bf16[2,1,64,256]{3,2,0,1:T(8,128)(2,1)S(1)}, u32[]{:S(2)}, u32[]{:S(2)}) collective-permute-start(bf16[2,1,64,256]{3,2,0,1:T(8,128)(2,1)S(1)} %fusion.48), channel_id=1, source_target_pairs={{0,16},{1,17},{2,18},{3,19},{4,20},{5,21},{6,22},{7,23},{8,24},{9,... | collective-permute-start | bytes 196616 | tf_op jit(solution)/shard_map/ppermute | solution.py:78
  277.6 5.7 %collective-permute-start.2 = (bf16[2,2,1,64,256]{4,3,1,0,2:T(8,128)(2,1)S(1)}, bf16[2,2,1,64,256]{4,3,1,0,2:T(8,128)(2,1)S(1)}, u32[]{:S(2)}, u32[]{:S(2)}) collective-permute-start(bf16[2,2,1,64,256]{4,3,1,0,2:T(8,128)(2,1)S(1)} %fusion.46), channel_id=1, source_target_pairs={{0,8},{1,9},{2,10},{3,11},{4,12},{5,13},{6,14},{7,15},{8,0},{9,1},... | collective-permute-start | bytes 393224 | tf_op jit(solution)/shard_map/ppermute | solution.py:78
  283.4 8.6 %collective-permute-start.3 = (bf16[2,2,2,1,64,256]{5,4,2,1,0,3:T(8,128)(2,1)S(1)}, bf16[2,2,2,1,64,256]{5,4,2,1,0,3:T(8,128)(2,1)S(1)}, u32[]{:S(2)}, u32[]{:S(2)}) collective-permute-start(bf16[2,2,2,1,64,256]{5,4,2,1,0,3:T(8,128)(2,1)S(1)} %fusion.34), channel_id=1, source_target_pairs={{0,4},{1,5},{2,6},{3,7},{4,0},{5,1},{6,2},{7,3},{8,12},{9,13},{10,... | collective-permute-start | bytes 786440 | tf_op jit(solution)/shard_map/ppermute | solution.py:78
  292.2 11.3 %collective-permute-start.4 = (bf16[2,2,2,2,1,64,256]{6,5,3,2,1,0,4:T(8,128)(2,1)S(1)}, bf16[2,2,2,2,1,64,256]{6,5,3,2,1,0,4:T(8,128)(2,1)S(1)}, u32[]{:S(2)}, u32[]{:S(2)}) collective-permute-start(bf16[2,2,2,2,1,64,256]{6,5,3,2,1,0,4:T(8,128)(2,1)S(1)} %fusion.32), channel_id=1, source_target_pairs={{0,2},{1,3},{2,0},{3,1},{4,6},{5,7},{6,4},{7,5},{8,10},{9,11},{10,... | collective-permute-start | bytes 1572872 | tf_op jit(solution)/shard_map/ppermute | solution.py:78
  304.7 9.4 %collective-permute-start.5 = (bf16[2,2,2,2,2,1,64,256]{7,6,4,3,2,1,0,5:T(8,128)(2,1)}, bf16[2,2,2,2,2,1,64,256]{7,6,4,3,2,1,0,5:T(8,128)(2,1)S(1)}, u32[]{:S(2)}, u32[]{:S(2)}) collective-permute-start(bf16[2,2,2,2,2,1,64,256]{7,6,4,3,2,1,0,5:T(8,128)(2,1)} %fusion.18), channel_id=1, source_target_pairs={{0,1},{1,0},{2,3},{3,2},{4,5},{5,4},{6,7},{7,6},{8,9},{9,8},{10,11... | collective-permute-start | bytes 3145736 | tf_op jit(solution)/shard_map/ppermute | solution.py:78
